TPU v7x, 32 devices: a whole 2x2x4 slice. The times are simulated.
32 devices in a mesh: freq: 32 (over z, y, x, core), tm: 1.
Axes of the slice: x: 2, y: 2, z: 4, core: 2. Of those that a mesh axis runs over, the one named last changes fastest.
Arguments:
- voltages: int32 [1024, 8, 2, 4096], P('freq', 'tm'), may hold values from -127 to 127
- tile_map: int32 [36], replicated, may hold values from 0 to 35, each once
Outputs:
- visibilities: float32 [36, 64, 2, 128, 128], P('tm', 'freq')
Inputs may be any that keep to these rules, and one draw needn't show every extreme that they name: `tile_map`: a permutation of the tile ids.
All inputs are finite; a program needn't handle non-finite values.
Results may differ from a plain program's by a relative error of at most 0.0052.
Values may be sent and summed in bfloat16 or wider, within the bound.
No kernel may reach another device: no remote copies, remote signals or barrier semaphores. Data moves between devices by JAX's collectives and lax.ppermute only.
A program may use at most 128 MiB of HBM per device.

v0:
```python
import math

import jax
import jax.numpy as jnp
from jax import lax
from jax.experimental import pallas as pl
from jax.experimental.pallas import tpu as pltpu
from jax.sharding import PartitionSpec as P

NCHAN = 4096
TAPS = 4
TB = 128
CH_DEV = 2
C_BLOCK = 512


def passed_along(value, axis, steps):
    count = lax.axis_size(axis)
    leading, last = (max(0, -steps), min(count, count - steps))
    return lax.ppermute(value, axis, [(source, source + steps) for source in range(leading, last)])


def prototype_rows():
    sample_idx = jnp.arange(TAPS * NCHAN, dtype=jnp.int32)
    position = (sample_idx.astype(jnp.float32) + 0.5) / NCHAN - TAPS / 2.0
    hann_taper = 0.5 - 0.5 * jnp.cos(
        (sample_idx.astype(jnp.float32) + 0.5) * (2.0 * math.pi / (TAPS * NCHAN))
    )
    return (jnp.sinc(position) * hann_taper / (128.0 * math.sqrt(NCHAN))).reshape(TAPS, NCHAN)


def channelize_kernel(first_channel, channels, proto_ref, x_ref, out_ref, acc_ref):
    step = pl.program_id(0)
    cb = x_ref.shape[-1]
    width = 2 * channels
    lane = lax.broadcasted_iota(jnp.int32, (cb, width), 1)
    sample = lax.broadcasted_iota(jnp.int32, (cb, width), 0) + step * cb
    upper = lane >= channels
    channel = first_channel + jnp.where(upper, lane - channels, lane)
    phase = (sample * channel) % NCHAN
    phase = jnp.where(upper, (phase + NCHAN // 4) % NCHAN, phase)
    cos_part = jnp.cos(phase.astype(jnp.float32) * (2.0 * math.pi / NCHAN))
    sin_part = pltpu.roll(cos_part, channels, 1) * jnp.where(upper, 1.0, -1.0).astype(jnp.float32)
    weights = proto_ref[...]
    re_tables = []
    im_tables = []
    for tap in range(TAPS):
        w = weights[:, tap : tap + 1]
        re_tables.append((w * cos_part).astype(jnp.bfloat16))
        im_tables.append((w * sin_part).astype(jnp.bfloat16))
    re_table = jnp.concatenate(re_tables, axis=1)
    im_table = jnp.concatenate(im_tables, axis=1)
    rows = x_ref.shape[0] * x_ref.shape[1]
    x_re = x_ref[:, :, 0, :].reshape(rows, cb).astype(jnp.bfloat16)
    x_im = x_ref[:, :, 1, :].reshape(rows, cb).astype(jnp.bfloat16)
    part = jnp.dot(x_re, re_table, preferred_element_type=jnp.float32) + jnp.dot(
        x_im, im_table, preferred_element_type=jnp.float32
    )

    @pl.when(step == 0)
    def _():
        acc_ref[...] = part

    @pl.when(step > 0)
    def _():
        acc_ref[...] += part

    @pl.when(step == pl.num_programs(0) - 1)
    def _():
        out_ref[...] = acc_ref[...]


def tap_products(voltages, proto_t, first_channel, channels):
    local_inputs, time_steps = voltages.shape[0], voltages.shape[1]
    rows = local_inputs * time_steps
    width = TAPS * 2 * channels
    blocks = NCHAN // C_BLOCK
    kernel = lambda *refs: channelize_kernel(first_channel, channels, *refs)
    return pl.pallas_call(
        kernel,
        out_shape=jax.ShapeDtypeStruct((rows, width), jnp.float32),
        grid=(blocks,),
        in_specs=[
            pl.BlockSpec((C_BLOCK, TAPS), lambda j: (j, 0)),
            pl.BlockSpec((local_inputs, time_steps, 2, C_BLOCK), lambda j: (0, 0, 0, j)),
        ],
        out_specs=pl.BlockSpec((rows, width), lambda j: (0, 0)),
        scratch_shapes=[pltpu.VMEM((rows, width), jnp.float32)],
        compiler_params=pltpu.CompilerParams(
            dimension_semantics=("arbitrary",), vmem_limit_bytes=48 * 1024 * 1024
        ),
        cost_estimate=pl.CostEstimate(
            flops=2 * rows * 2 * NCHAN * width,
            transcendentals=NCHAN * 2 * channels,
            bytes_accessed=voltages.size * 4 + rows * width * 4,
        ),
    )(proto_t, voltages)


def tile_coords(tile_id, blocks):
    step_row = jnp.arange(1, blocks, dtype=jnp.int32)
    triangle = step_row * (step_row + 1) // 2
    row_block = jnp.sum((tile_id[..., None] >= triangle).astype(jnp.int32), axis=-1)
    col_block = tile_id - row_block * (row_block + 1) // 2
    return (row_block, col_block)


def arrange_rows(gathered, time_steps):
    piece_count = gathered.shape[0]
    freq_count = gathered.shape[1]
    local_chans = gathered.shape[2]
    inner_width = gathered.shape[4] // time_steps
    unfolded = gathered.reshape(piece_count, freq_count, local_chans, 2, time_steps, inner_width)
    unfolded = unfolded.transpose(2, 3, 0, 4, 1, 5)
    return unfolded.reshape(local_chans, 2, piece_count * time_steps, freq_count * inner_width)


def tile_products(spectra, tile_ids):
    blocks = spectra.shape[3] // TB
    row_block, col_block = tile_coords(tile_ids, blocks)
    shaped = spectra.reshape(spectra.shape[0], 2, spectra.shape[2], blocks, TB)
    row_tiles = jnp.take(shaped, row_block, axis=3)
    col_tiles = jnp.take(shaped, col_block, axis=3)
    turned = jnp.stack([row_tiles[:, 1], -row_tiles[:, 0]], axis=1)
    paired = jnp.stack([row_tiles, turned], axis=1)
    return jnp.einsum("hqptsx,hptsy->shqxy", paired, col_tiles, preferred_element_type=jnp.float32)


def on_device(voltages, tile_map):
    local_inputs = voltages.shape[0]
    time_steps = voltages.shape[1]
    freq_devices = lax.axis_size("freq")
    time_devices = lax.axis_size("tm")
    channels = CH_DEV * freq_devices
    first_channel = NCHAN // 2 - channels // 2
    proto_t = prototype_rows().T
    products = tap_products(voltages, proto_t, first_channel, channels)
    products = products.reshape(local_inputs, time_steps, TAPS, 2, channels)
    tail = products[:, time_steps - (TAPS - 1) :]
    if time_devices > 1:
        previous = passed_along(tail, "tm", 1)
    else:
        previous = jnp.zeros_like(tail)
    total = None
    for tap in range(TAPS):
        lead = TAPS - 1 - tap
        shifted = jnp.concatenate(
            [previous[:, tap:, tap], products[:, : time_steps - lead, tap]], axis=1
        )
        total = shifted if total is None else total + shifted
    spectra = total.astype(jnp.bfloat16)
    spectra = spectra.reshape(local_inputs, time_steps, 2, freq_devices, CH_DEV)
    spectra = spectra.transpose(3, 4, 2, 1, 0).reshape(
        freq_devices, CH_DEV, 2, time_steps * local_inputs
    )
    turned = lax.all_to_all(spectra, "freq", split_axis=0, concat_axis=0, tiled=True)
    slot_count = tile_map.shape[0] // time_devices
    inverse_count = 1.0 / (time_steps * time_devices)
    tile_ids = lax.dynamic_slice_in_dim(tile_map, lax.axis_index("tm") * slot_count, slot_count)
    summed = tile_products(
        arrange_rows(lax.all_gather(turned[None], "tm", axis=0, tiled=True), time_steps), tile_ids
    )
    return summed * inverse_count


def solution(mesh):
    in_specs = (P("freq", "tm", None, None), P())
    out_specs = P("tm", "freq", None, None, None)
    return jax.shard_map(
        on_device, mesh=mesh, in_specs=in_specs, out_specs=out_specs, check_vma=False
    )
```

profile of v0, /device:TPU:0, one launch (start us, length us, event | category | flops | bytes accessed | tf_op | source)
XLA Modules:
  0.0 60.1 jit_solution(14709257294997383073)
XLA Ops:
  0.0 9.6 %fusion.13.refs_0_ = f32[4096,4]{1,0:T(8,128)S(1)} fusion(), kind=kLoop, calls=%fused_computation.27 | loop fusion | flops 720896 | bytes 65536 | tf_op jit(solution)/shard_map/div | solution.py:29
  9.6 25.7 %shard_map.28 = f32[256,512]{1,0:T(8,128)S(1)} custom-call(f32[4096,4]{1,0:T(8,128)S(1)} %fusion.13.refs_0_, s32[32,8,2,4096]{3,2,1,0:T(2,128)} %refs_1_.1), custom_call_target="tpu_custom_call" | custom-call | flops 2147483648 | bytes 8912896 | tf_op jit(solution)/shard_map/pallas_call | solution.py:79
  35.3 0.8 %reshape.43 = f32[32,8,4,2,64]{4,3,2,1,0:T(2,128)S(1)} reshape(f32[256,512]{1,0:T(8,128)S(1)} %shard_map.28) | data formatting | bytes 1048576 | tf_op jit(solution)/shard_map/reshape | solution.py:138
  36.0 0.1 slice.28
  36.1 0.1 slice.29
  36.2 0.1 slice.30
  36.3 0.1 slice.31
  36.4 0.3 copy.53
  36.7 0.3 copy.52
  36.9 0.0 copy-start
  36.9 0.3 copy.51
  37.2 0.3 copy.50
  37.5 0.3 fusion.17
  37.7 0.2 reshape.71
  37.9 0.7 %copy.41 = bf16[32,2,2,256]{3,2,1,0:T(2,128)(2,1)} copy(bf16[32,2,2,256]{3,1,0,2:T(2,128)(2,1)S(1)} %reshape.71) | data formatting | bytes 131072 | tf_op jit(solution)/shard_map/reshape | solution.py:153
  38.6 7.3 %all-to-all-start = ((bf16[32,2,2,256]{3,2,1,0:T(2,128)(2,1)}), bf16[32,2,2,256]{3,2,1,0:T(2,128)(2,1)S(1)}, u32[]{:S(2)}, u32[]{:S(2)}) async-start(bf16[32,2,2,256]{3,2,1,0:T(2,128)(2,1)} %copy.41), calls=%async_computation | async-start | bytes 131072 | tf_op jit(solution)/shard_map/all_to_all | solution.py:156
  46.0 0.0 copy-done
  46.0 0.1 convert_reduce_fusion
  46.1 7.2 %all-to-all-done = bf16[32,2,2,256]{3,2,1,0:T(2,128)(2,1)S(1)} async-done(((bf16[32,2,2,256]{3,2,1,0:T(2,128)(2,1)}), bf16[32,2,2,256]{3,2,1,0:T(2,128)(2,1)S(1)}, u32[]{:S(2)}, u32[]{:S(2)}) %all-to-all-start) | async-done | bytes 65568 | tf_op jit(solution)/shard_map/all_to_all | solution.py:156
  53.4 0.2 reshape.46
  53.5 0.1 copy.55
  53.7 0.2 reshape_reshape.3
  53.9 0.7 %gather_fusion.1 = bf16[36,2,2,8,128]{4,3,2,1,0:T(8,128)(2,1)S(1)} fusion(bf16[2,2,8,8,128]{4,2,3,1,0:T(8,128)(2,1)S(1)} %copy.43, s32[1024]{0:T(1024)S(1)} %pad_clamp_fusion), kind=kCustom, calls=%fused_computation.1.clone | custom fusion | bytes 589968 | tf_op jit(solution)/shard_map/jit(_take)/gather | solution.py:123
  54.5 0.7 %gather_fusion = bf16[36,2,2,8,128]{4,3,2,1,0:T(8,128)(2,1)S(1)} fusion(bf16[2,2,8,8,128]{4,2,3,1,0:T(8,128)(2,1)S(1)} %copy.43, s32[1024]{0:T(1024)S(1)} %pad_clamp_fusion.1), kind=kCustom, calls=%fused_computation.clone | custom fusion | bytes 589968 | tf_op jit(solution)/shard_map/jit(_take)/gather | solution.py:122
  55.2 0.1 fusion.22
  55.4 0.1 maximum_bitcast_fusion
  55.4 4.7 %bitcast_multiply_fusion = f32[36,2,2,128,128]{4,3,2,1,0:T(8,128)} fusion(bf16[2,1,2,8,36,128]{5,3,2,1,0,4:T(8,128)(2,1)S(1)} %maximum_bitcast_fusion, bf16[2,1,2,8,36,128]{5,3,2,1,0,4:T(8,128)(2,1)S(1)} %get-tuple-element.8, bf16[36,2,2,8,128]{4,3,2,1,0:T(8,128)(2,1)S(1)} %gather_fusion.1, pred[36]{0:T(512)(128)(4,1)S(1)} %get-tuple-element.6), kind=kOutput, calls=%fused_computation.2 | convolution fusion | flops 78299136 | bytes 10321956 | tf_op jit(solution)/shard_map/hqptsx,hptsy->shqxy/dot_general | solution.py:126
  (7 shorter events, 0.1 us)
Async XLA Ops:
  36.9 9.0 %copy-start = (s32[36]{0:T(128)S(1)}, s32[36]{0:T(128)}, u32[]{:S(2)}) copy-start(s32[36]{0:T(128)} %param.5) | copy-start | bytes 436
  38.6 14.7 %all-to-all-start = ((bf16[32,2,2,256]{3,2,1,0:T(2,128)(2,1)}), bf16[32,2,2,256]{3,2,1,0:T(2,128)(2,1)S(1)}, u32[]{:S(2)}, u32[]{:S(2)}) async-start(bf16[32,2,2,256]{3,2,1,0:T(2,128)(2,1)} %copy.41), calls=%async_computation | async-start | bytes 131072 | tf_op jit(solution)/shard_map/all_to_all | solution.py:156
where the time goes:
time: 60.3 us; the launch traced here: 60.1 us
  Pallas kernels  25.7 us (43%)
  other arithmetic  10.2 us (17%)
  starting transfers between devices  7.33 us (12%)
  waiting for transfers between devices  7.24 us (12%)
  local copies, waits for them, and re-layouts  4.75 us (8%)
  matrix products  4.65 us (8%)
    pallas_call x1, Pallas kernels, tap_products(): pl.pallas_call(kernel, out_shape=jax.ShapeDtypeStruct((rows, width), jnp....  25.7 us
    div x1, other arithmetic, prototype_rows(): jnp.sinc(position) * hann_taper / (128.0 * math.sqrt(NCHAN))  9.59 us
    all_to_all x1, starting transfers between devices, on_device(): lax.all_to_all(spectra, 'freq', split_axis=0, concat_axis=0, tiled=True)  7.33 us
    all_to_all x1, waiting for transfers between devices, on_device(): lax.all_to_all(spectra, 'freq', split_axis=0, concat_axis=0, tiled=True)  7.24 us
    dot_general x1, matrix products, tile_products(): jnp.einsum('hqptsx,hptsy->shqxy', paired, col_tiles, preferred_element_ty...  4.65 us
  transfers between devices with their start and end apart: 1, of which 1 were waited for; matrix products, arithmetic and copies ran while one was open for 0% of the time, Pallas kernels for 0%

commit v1 on v0

--- a/solution.py
+++ b/solution.py
@@ -29,32 +29,40 @@
     return (jnp.sinc(position) * hann_taper / (128.0 * math.sqrt(NCHAN))).reshape(TAPS, NCHAN)
 
 
-def channelize_kernel(first_channel, channels, proto_ref, x_ref, out_ref, acc_ref):
+def phase_table(first_channel, channels):
+    radix = 64
+    channel = first_channel + jnp.arange(channels, dtype=jnp.int32)
+    digit = jnp.arange(radix, dtype=jnp.int32)
+    step = 2.0 * math.pi / NCHAN
+    high = ((digit[None, :] * radix * channel[:, None]) % NCHAN).astype(jnp.float32) * step
+    low = ((digit[None, :] * channel[:, None]) % NCHAN).astype(jnp.float32) * step
+    cos_hi, sin_hi = jnp.cos(high)[:, :, None], jnp.sin(high)[:, :, None]
+    cos_lo, sin_lo = jnp.cos(low)[:, None, :], jnp.sin(low)[:, None, :]
+    cosine = (cos_hi * cos_lo - sin_hi * sin_lo).reshape(channels, NCHAN)
+    sine = (sin_hi * cos_lo + cos_hi * sin_lo).reshape(channels, NCHAN)
+    return jnp.concatenate([cosine, -sine], axis=0)
+
+
+def channelize_kernel(channels, proto_ref, phase_ref, x_ref, out_ref, acc_ref):
     step = pl.program_id(0)
     cb = x_ref.shape[-1]
-    width = 2 * channels
-    lane = lax.broadcasted_iota(jnp.int32, (cb, width), 1)
-    sample = lax.broadcasted_iota(jnp.int32, (cb, width), 0) + step * cb
-    upper = lane >= channels
-    channel = first_channel + jnp.where(upper, lane - channels, lane)
-    phase = (sample * channel) % NCHAN
-    phase = jnp.where(upper, (phase + NCHAN // 4) % NCHAN, phase)
-    cos_part = jnp.cos(phase.astype(jnp.float32) * (2.0 * math.pi / NCHAN))
-    sin_part = pltpu.roll(cos_part, channels, 1) * jnp.where(upper, 1.0, -1.0).astype(jnp.float32)
+    upper = phase_ref[...]
+    lower = jnp.concatenate([-upper[channels:], upper[:channels]], axis=0)
     weights = proto_ref[...]
     re_tables = []
     im_tables = []
     for tap in range(TAPS):
-        w = weights[:, tap : tap + 1]
-        re_tables.append((w * cos_part).astype(jnp.bfloat16))
-        im_tables.append((w * sin_part).astype(jnp.bfloat16))
-    re_table = jnp.concatenate(re_tables, axis=1)
-    im_table = jnp.concatenate(im_tables, axis=1)
+        w = weights[tap : tap + 1, :]
+        re_tables.append((w * upper).astype(jnp.bfloat16))
+        im_tables.append((w * lower).astype(jnp.bfloat16))
+    re_table = jnp.concatenate(re_tables, axis=0)
+    im_table = jnp.concatenate(im_tables, axis=0)
     rows = x_ref.shape[0] * x_ref.shape[1]
     x_re = x_ref[:, :, 0, :].reshape(rows, cb).astype(jnp.bfloat16)
     x_im = x_ref[:, :, 1, :].reshape(rows, cb).astype(jnp.bfloat16)
-    part = jnp.dot(x_re, re_table, preferred_element_type=jnp.float32) + jnp.dot(
-        x_im, im_table, preferred_element_type=jnp.float32
+    dims = (((1,), (1,)), ((), ()))
+    part = lax.dot_general(x_re, re_table, dims, preferred_element_type=jnp.float32) + lax.dot_general(
+        x_im, im_table, dims, preferred_element_type=jnp.float32
     )
 
     @pl.when(step == 0)
@@ -70,18 +78,19 @@
         out_ref[...] = acc_ref[...]
 
 
-def tap_products(voltages, proto_t, first_channel, channels):
+def tap_products(voltages, proto, phase, channels):
     local_inputs, time_steps = voltages.shape[0], voltages.shape[1]
     rows = local_inputs * time_steps
     width = TAPS * 2 * channels
     blocks = NCHAN // C_BLOCK
-    kernel = lambda *refs: channelize_kernel(first_channel, channels, *refs)
+    kernel = lambda *refs: channelize_kernel(channels, *refs)
     return pl.pallas_call(
         kernel,
         out_shape=jax.ShapeDtypeStruct((rows, width), jnp.float32),
         grid=(blocks,),
         in_specs=[
-            pl.BlockSpec((C_BLOCK, TAPS), lambda j: (j, 0)),
+            pl.BlockSpec((TAPS, C_BLOCK), lambda j: (0, j)),
+            pl.BlockSpec((2 * channels, C_BLOCK), lambda j: (0, j)),
             pl.BlockSpec((local_inputs, time_steps, 2, C_BLOCK), lambda j: (0, 0, 0, j)),
         ],
         out_specs=pl.BlockSpec((rows, width), lambda j: (0, 0)),
@@ -91,10 +100,10 @@
         ),
         cost_estimate=pl.CostEstimate(
             flops=2 * rows * 2 * NCHAN * width,
-            transcendentals=NCHAN * 2 * channels,
-            bytes_accessed=voltages.size * 4 + rows * width * 4,
+            transcendentals=0,
+            bytes_accessed=voltages.size * 4 + rows * width * 4 + phase.size * 4,
         ),
-    )(proto_t, voltages)
+    )(proto, phase, voltages)
 
 
 def tile_coords(tile_id, blocks):
@@ -133,8 +142,9 @@
     time_devices = lax.axis_size("tm")
     channels = CH_DEV * freq_devices
     first_channel = NCHAN // 2 - channels // 2
-    proto_t = prototype_rows().T
-    products = tap_products(voltages, proto_t, first_channel, channels)
+    proto = prototype_rows()
+    phase = phase_table(first_channel, channels)
+    products = tap_products(voltages, proto, phase, channels)
     products = products.reshape(local_inputs, time_steps, TAPS, 2, channels)
     tail = products[:, time_steps - (TAPS - 1) :]
     if time_devices > 1:

time: 60.3 us -> 48 us (0.80)
  Pallas kernels: 25.7 us -> 14.6 us
  other arithmetic: 10.2 us -> 5.17 us
  local copies, waits for them, and re-layouts: 4.75 us -> 8.5 us
    pallas_call x1, Pallas kernels: 25.7 us -> 14.6 us  [tap_products(): pl.pallas_call(kernel, out_shape=jax.ShapeDtypeStruct((rows, width), jnp....]
    div x1, other arithmetic: 9.59 us -> 0.62 us  [prototype_rows(): jnp.sinc(position) * hann_taper / (128.0 * math.sqrt(NCHAN))]
    sub x0 -> x1, other arithmetic: none -> 2.22 us  [phase_table(): cosine = (cos_hi * cos_lo - sin_hi * sin_lo).reshape(channels, NCHAN)]
    sub x0 -> x1, local copies, waits for them, and re-layouts: none -> 2.12 us  [phase_table(): cosine = (cos_hi * cos_lo - sin_hi * sin_lo).reshape(channels, NCHAN)]
    neg x0 -> x1, local copies, waits for them, and re-layouts: none -> 1.62 us  [phase_table(): return jnp.concatenate([cosine, -sine], axis=0)]
    concatenate x0 -> x1, other arithmetic: none -> 1.37 us  [phase_table(): return jnp.concatenate([cosine, -sine], axis=0)]
where the time goes in v1:
time: 48 us; the launch traced here: 47.8 us
  Pallas kernels  14.6 us (30%)
  local copies, waits for them, and re-layouts  8.5 us (18%)
  starting transfers between devices  7.33 us (15%)
  waiting for transfers between devices  7.24 us (15%)
  other arithmetic  5.17 us (11%)
  matrix products  4.65 us (10%)
    pallas_call x1, Pallas kernels, tap_products(): pl.pallas_call(kernel, out_shape=jax.ShapeDtypeStruct((rows, width), jnp....  14.6 us
    all_to_all x1, starting transfers between devices, on_device(): lax.all_to_all(spectra, 'freq', split_axis=0, concat_axis=0, tiled=True)  7.33 us
    all_to_all x1, waiting for transfers between devices, on_device(): lax.all_to_all(spectra, 'freq', split_axis=0, concat_axis=0, tiled=True)  7.24 us
    dot_general x1, matrix products, tile_products(): jnp.einsum('hqptsx,hptsy->shqxy', paired, col_tiles, preferred_element_ty...  4.65 us
    sub x1, other arithmetic, phase_table(): cosine = (cos_hi * cos_lo - sin_hi * sin_lo).reshape(channels, NCHAN)  2.22 us
    sub x1, local copies, waits for them, and re-layouts, phase_table(): cosine = (cos_hi * cos_lo - sin_hi * sin_lo).reshape(channels, NCHAN)  2.12 us
    neg x1, local copies, waits for them, and re-layouts, phase_table(): return jnp.concatenate([cosine, -sine], axis=0)  1.62 us
    concatenate x1, other arithmetic, phase_table(): return jnp.concatenate([cosine, -sine], axis=0)  1.37 us
  transfers between devices with their start and end apart: 1, of which 1 were waited for; matrix products, arithmetic and copies ran while one was open for 0% of the time, Pallas kernels for 0%

profile of v1, /device:TPU:0, one launch (start us, length us, event | category | flops | bytes accessed | tf_op | source)
XLA Modules:
  0.0 47.8 jit_solution(6162910981329083828)
XLA Ops:
  0.0 0.6 %fusion.16.refs_0_ = f32[4,4096]{1,0:T(4,128)S(1)} fusion(), kind=kLoop, calls=%fused_computation.33 | loop fusion | flops 720896 | bytes 65536 | tf_op jit(solution)/shard_map/div | solution.py:29
  0.6 0.3 fusion.34
  1.0 2.2 %multiply_subtract_fusion = (f32[64,64,64]{2,1,0:T(8,128)}, f32[64,64,64]{2,1,0:T(8,128)S(1)}) fusion(f32[64,64]{1,0:T(8,128)S(1)} %get-tuple-element.17, f32[64,64]{1,0:T(8,128)S(1)} %get-tuple-element.15, f32[64,64]{1,0:T(8,128)S(1)} %get-tuple-element.18, f32[64,64]{1,0:T(8,128)S(1)} %get-tuple-element.14), kind=kLoop, calls=%fused_computation.5 | loop fusion | flops 1835008 | bytes 2162688 | tf_op jit(solution)/shard_map/sub | solution.py:41
  3.2 2.1 %sub.46 = f32[64,4096]{1,0:T(8,128)S(1)} reshape(f32[64,64,64]{2,1,0:T(8,128)} %get-tuple-element.12) | data formatting | bytes 2097152 | tf_op jit(solution)/shard_map/sub | solution.py:41
  5.3 1.6 %neg.17 = f32[64,4096]{1,0:T(8,128)} reshape(f32[64,64,64]{2,1,0:T(8,128)S(1)} %get-tuple-element.13) | data formatting | bytes 2097152 | tf_op jit(solution)/shard_map/neg | solution.py:43
  6.9 1.4 %pad_maximum_fusion.refs_1_ = f32[128,4096]{1,0:T(8,128)S(1)} fusion(f32[64,4096]{1,0:T(8,128)} %neg.17, f32[64,4096]{1,0:T(8,128)S(1)} %sub.46), kind=kLoop, calls=%fused_computation.3 | loop fusion | flops 524288 | bytes 4194304 | tf_op jit(solution)/shard_map/concatenate | solution.py:43
  8.3 14.6 %shard_map.28 = f32[256,512]{1,0:T(8,128)S(1)} custom-call(f32[4,4096]{1,0:T(4,128)S(1)} %fusion.16.refs_0_, f32[128,4096]{1,0:T(8,128)S(1)} %pad_maximum_fusion.refs_1_, s32[32,8,2,4096]{3,2,1,0:T(2,128)} %refs_2_.1), custom_call_target="tpu_custom_call" | custom-call | flops 2147483648 | bytes 11010048 | tf_op jit(solution)/shard_map/pallas_call | solution.py:87
  23.0 0.8 %reshape.184 = f32[32,8,4,2,64]{4,3,2,1,0:T(2,128)S(1)} reshape(f32[256,512]{1,0:T(8,128)S(1)} %shard_map.28) | data formatting | bytes 1048576 | tf_op jit(solution)/shard_map/reshape | solution.py:148
  23.7 0.1 slice.28
  23.8 0.1 slice.29
  23.9 0.1 slice.30
  24.0 0.1 slice.31
  24.1 0.3 copy.43
  24.4 0.3 copy.42
  24.6 0.0 copy-start
  24.6 0.3 copy.41
  24.9 0.3 copy.40
  25.1 0.3 fusion.3
  25.4 0.2 reshape.212
  25.6 0.7 %copy.31 = bf16[32,2,2,256]{3,2,1,0:T(2,128)(2,1)} copy(bf16[32,2,2,256]{3,1,0,2:T(2,128)(2,1)S(1)} %reshape.212) | data formatting | bytes 131072 | tf_op jit(solution)/shard_map/reshape | solution.py:163
  26.3 7.3 %all-to-all-start = ((bf16[32,2,2,256]{3,2,1,0:T(2,128)(2,1)}), bf16[32,2,2,256]{3,2,1,0:T(2,128)(2,1)S(1)}, u32[]{:S(2)}, u32[]{:S(2)}) async-start(bf16[32,2,2,256]{3,2,1,0:T(2,128)(2,1)} %copy.31), calls=%async_computation | async-start | bytes 131072 | tf_op jit(solution)/shard_map/all_to_all | solution.py:166
  33.7 0.0 copy-done
  33.7 0.1 convert_reduce_fusion
  33.8 7.2 %all-to-all-done = bf16[32,2,2,256]{3,2,1,0:T(2,128)(2,1)S(1)} async-done(((bf16[32,2,2,256]{3,2,1,0:T(2,128)(2,1)}), bf16[32,2,2,256]{3,2,1,0:T(2,128)(2,1)S(1)}, u32[]{:S(2)}, u32[]{:S(2)}) %all-to-all-start) | async-done | bytes 65568 | tf_op jit(solution)/shard_map/all_to_all | solution.py:166
  41.1 0.2 reshape.187
  41.2 0.1 copy.45
  41.4 0.2 reshape_reshape.3
  41.5 0.7 %gather_fusion.1 = bf16[36,2,2,8,128]{4,3,2,1,0:T(8,128)(2,1)S(1)} fusion(bf16[2,2,8,8,128]{4,2,3,1,0:T(8,128)(2,1)S(1)} %copy.33, s32[1024]{0:T(1024)S(1)} %pad_clamp_fusion), kind=kCustom, calls=%fused_computation.1.clone | custom fusion | bytes 589968 | tf_op jit(solution)/shard_map/jit(_take)/gather | solution.py:132
  42.2 0.7 %gather_fusion = bf16[36,2,2,8,128]{4,3,2,1,0:T(8,128)(2,1)S(1)} fusion(bf16[2,2,8,8,128]{4,2,3,1,0:T(8,128)(2,1)S(1)} %copy.33, s32[1024]{0:T(1024)S(1)} %pad_clamp_fusion.1), kind=kCustom, calls=%fused_computation.clone | custom fusion | bytes 589968 | tf_op jit(solution)/shard_map/jit(_take)/gather | solution.py:131
  42.9 0.1 fusion.8
  43.0 0.1 maximum_bitcast_fusion
  43.1 4.7 %bitcast_multiply_fusion = f32[36,2,2,128,128]{4,3,2,1,0:T(8,128)} fusion(bf16[2,1,2,8,36,128]{5,3,2,1,0,4:T(8,128)(2,1)S(1)} %maximum_bitcast_fusion, bf16[2,1,2,8,36,128]{5,3,2,1,0,4:T(8,128)(2,1)S(1)} %get-tuple-element.8, bf16[36,2,2,8,128]{4,3,2,1,0:T(8,128)(2,1)S(1)} %gather_fusion.1, pred[36]{0:T(512)(128)(4,1)S(1)} %get-tuple-element.6), kind=kOutput, calls=%fused_computation.2 | convolution fusion | flops 78299136 | bytes 10321956 | tf_op jit(solution)/shard_map/hqptsx,hptsy->shqxy/dot_general | solution.py:135
  (8 shorter events, 0.1 us)
Async XLA Ops:
  24.6 9.0 %copy-start = (s32[36]{0:T(128)S(1)}, s32[36]{0:T(128)}, u32[]{:S(2)}) copy-start(s32[36]{0:T(128)} %param.5) | copy-start | bytes 436
  26.3 14.7 %all-to-all-start = ((bf16[32,2,2,256]{3,2,1,0:T(2,128)(2,1)}), bf16[32,2,2,256]{3,2,1,0:T(2,128)(2,1)S(1)}, u32[]{:S(2)}, u32[]{:S(2)}) async-start(bf16[32,2,2,256]{3,2,1,0:T(2,128)(2,1)} %copy.31), calls=%async_computation | async-start | bytes 131072 | tf_op jit(solution)/shard_map/all_to_all | solution.py:166

commit v2 on v1

--- a/solution.py
+++ b/solution.py
@@ -29,25 +29,49 @@
     return (jnp.sinc(position) * hann_taper / (128.0 * math.sqrt(NCHAN))).reshape(TAPS, NCHAN)
 
 
-def phase_table(first_channel, channels):
-    radix = 64
+def phase_tables(first_channel, channels):
     channel = first_channel + jnp.arange(channels, dtype=jnp.int32)
-    digit = jnp.arange(radix, dtype=jnp.int32)
     step = 2.0 * math.pi / NCHAN
-    high = ((digit[None, :] * radix * channel[:, None]) % NCHAN).astype(jnp.float32) * step
-    low = ((digit[None, :] * channel[:, None]) % NCHAN).astype(jnp.float32) * step
-    cos_hi, sin_hi = jnp.cos(high)[:, :, None], jnp.sin(high)[:, :, None]
-    cos_lo, sin_lo = jnp.cos(low)[:, None, :], jnp.sin(low)[:, None, :]
-    cosine = (cos_hi * cos_lo - sin_hi * sin_lo).reshape(channels, NCHAN)
-    sine = (sin_hi * cos_lo + cos_hi * sin_lo).reshape(channels, NCHAN)
-    return jnp.concatenate([cosine, -sine], axis=0)
-
-
-def channelize_kernel(channels, proto_ref, phase_ref, x_ref, out_ref, acc_ref):
+    lane = jnp.arange(C_BLOCK, dtype=jnp.int32)
+    start = ((lane[None, :] * channel[:, None]) % NCHAN).astype(jnp.float32) * step
+    first = jnp.concatenate([jnp.cos(start), jnp.sin(start)], axis=0)
+    block = jnp.arange(NCHAN // C_BLOCK, dtype=jnp.int32) * C_BLOCK
+    shift = ((block[:, None] * channel[None, :]) % NCHAN).astype(jnp.float32) * step
+    turn = jnp.concatenate([jnp.cos(shift), jnp.sin(shift)], axis=1)
+    return first, jnp.broadcast_to(turn[:, :, None], turn.shape + (128,))
+
+
+def channelize_kernel(channels, proto_ref, first_ref, turn_ref, x_hbm, out_ref, buf, sems, acc_ref):
     step = pl.program_id(0)
-    cb = x_ref.shape[-1]
-    upper = phase_ref[...]
-    lower = jnp.concatenate([-upper[channels:], upper[:channels]], axis=0)
+    count = pl.num_programs(0)
+    cb = buf.shape[-1]
+
+    def fetch(block, slot):
+        for part in range(2):
+            pltpu.make_async_copy(
+                x_hbm.at[:, :, part, pl.ds(block * cb, cb)], buf.at[slot, part], sems.at[slot, part]
+            ).start()
+
+    @pl.when(step == 0)
+    def _():
+        fetch(0, 0)
+
+    @pl.when(step + 1 < count)
+    def _():
+        fetch(step + 1, (step + 1) % 2)
+
+    slot = step % 2
+    for part in range(2):
+        pltpu.make_async_copy(
+            x_hbm.at[:, :, part, pl.ds(0, cb)], buf.at[slot, part], sems.at[slot, part]
+        ).wait()
+    turn = jnp.concatenate([turn_ref[...]] * (cb // turn_ref.shape[-1]), axis=1)
+    cos_0, sin_0 = first_ref[:channels], first_ref[channels:]
+    cos_t, sin_t = turn[:channels], turn[channels:]
+    cosine = cos_0 * cos_t - sin_0 * sin_t
+    sine = sin_0 * cos_t + cos_0 * sin_t
+    upper = jnp.concatenate([cosine, -sine], axis=0)
+    lower = jnp.concatenate([sine, cosine], axis=0)
     weights = proto_ref[...]
     re_tables = []
     im_tables = []
@@ -57,9 +81,9 @@
         im_tables.append((w * lower).astype(jnp.bfloat16))
     re_table = jnp.concatenate(re_tables, axis=0)
     im_table = jnp.concatenate(im_tables, axis=0)
-    rows = x_ref.shape[0] * x_ref.shape[1]
-    x_re = x_ref[:, :, 0, :].reshape(rows, cb).astype(jnp.bfloat16)
-    x_im = x_ref[:, :, 1, :].reshape(rows, cb).astype(jnp.bfloat16)
+    rows = buf.shape[2] * buf.shape[3]
+    x_re = buf[slot, 0].reshape(rows, cb).astype(jnp.bfloat16)
+    x_im = buf[slot, 1].reshape(rows, cb).astype(jnp.bfloat16)
     dims = (((1,), (1,)), ((), ()))
     part = lax.dot_general(x_re, re_table, dims, preferred_element_type=jnp.float32) + lax.dot_general(
         x_im, im_table, dims, preferred_element_type=jnp.float32
@@ -78,7 +102,7 @@
         out_ref[...] = acc_ref[...]
 
 
-def tap_products(voltages, proto, phase, channels):
+def tap_products(voltages, proto, first, turn, channels):
     local_inputs, time_steps = voltages.shape[0], voltages.shape[1]
     rows = local_inputs * time_steps
     width = TAPS * 2 * channels
@@ -90,20 +114,25 @@
         grid=(blocks,),
         in_specs=[
             pl.BlockSpec((TAPS, C_BLOCK), lambda j: (0, j)),
-            pl.BlockSpec((2 * channels, C_BLOCK), lambda j: (0, j)),
-            pl.BlockSpec((local_inputs, time_steps, 2, C_BLOCK), lambda j: (0, 0, 0, j)),
+            pl.BlockSpec((2 * channels, C_BLOCK), lambda j: (0, 0)),
+            pl.BlockSpec((None, 2 * channels, 128), lambda j: (j, 0, 0)),
+            pl.BlockSpec(memory_space=pl.ANY),
         ],
         out_specs=pl.BlockSpec((rows, width), lambda j: (0, 0)),
-        scratch_shapes=[pltpu.VMEM((rows, width), jnp.float32)],
+        scratch_shapes=[
+            pltpu.VMEM((2, 2, local_inputs, time_steps, C_BLOCK), jnp.int32),
+            pltpu.SemaphoreType.DMA((2, 2)),
+            pltpu.VMEM((rows, width), jnp.float32),
+        ],
         compiler_params=pltpu.CompilerParams(
             dimension_semantics=("arbitrary",), vmem_limit_bytes=48 * 1024 * 1024
         ),
         cost_estimate=pl.CostEstimate(
             flops=2 * rows * 2 * NCHAN * width,
             transcendentals=0,
-            bytes_accessed=voltages.size * 4 + rows * width * 4 + phase.size * 4,
+            bytes_accessed=voltages.size * 4 + rows * width * 4 + first.size * 4 + turn.size * 4,
         ),
-    )(proto, phase, voltages)
+    )(proto, first, turn, voltages)
 
 
 def tile_coords(tile_id, blocks):
@@ -143,8 +172,8 @@
     channels = CH_DEV * freq_devices
     first_channel = NCHAN // 2 - channels // 2
     proto = prototype_rows()
-    phase = phase_table(first_channel, channels)
-    products = tap_products(voltages, proto, phase, channels)
+    first, turn = phase_tables(first_channel, channels)
+    products = tap_products(voltages, proto, first, turn, channels)
     products = products.reshape(local_inputs, time_steps, TAPS, 2, channels)
     tail = products[:, time_steps - (TAPS - 1) :]
     if time_devices > 1:

time: 48 us -> 34.9 us (0.73)
  Pallas kernels: 14.6 us -> 8.17 us
  local copies, waits for them, and re-layouts: 8.5 us -> 4.95 us
  other arithmetic: 5.17 us -> 2.05 us
    pallas_call x1, Pallas kernels: 14.6 us -> 8.17 us  [tap_products(): pl.pallas_call(kernel, out_shape=jax.ShapeDtypeStruct((rows, width), jnp....]
    sub x1 -> x0, other arithmetic: 2.22 us -> none  [phase_table(): cosine = (cos_hi * cos_lo - sin_hi * sin_lo).reshape(channels, NCHAN)]
    sub x1 -> x0, local copies, waits for them, and re-layouts: 2.12 us -> none  [phase_table(): cosine = (cos_hi * cos_lo - sin_hi * sin_lo).reshape(channels, NCHAN)]
    neg x1 -> x0, local copies, waits for them, and re-layouts: 1.62 us -> none  [phase_table(): return jnp.concatenate([cosine, -sine], axis=0)]
    concatenate x1 -> x2, other arithmetic: 1.37 us -> 0.1 us  [the longest x1 0.08 us: phase_tables(): turn = jnp.concatenate([jnp.cos(shift), jnp.sin(shift)], axis=1)]
where the time goes in v2:
time: 34.9 us; the launch traced here: 34.6 us
  Pallas kernels  8.17 us (23%)
  starting transfers between devices  7.31 us (21%)
  waiting for transfers between devices  7.24 us (21%)
  local copies, waits for them, and re-layouts  4.95 us (14%)
  matrix products  4.65 us (13%)
  other arithmetic  2.05 us (6%)
    pallas_call x1, Pallas kernels, tap_products(): pl.pallas_call(kernel, out_shape=jax.ShapeDtypeStruct((rows, width), jnp....  8.17 us
    all_to_all x1, starting transfers between devices, on_device(): lax.all_to_all(spectra, 'freq', split_axis=0, concat_axis=0, tiled=True)  7.31 us
    all_to_all x1, waiting for transfers between devices, on_device(): lax.all_to_all(spectra, 'freq', split_axis=0, concat_axis=0, tiled=True)  7.24 us
    dot_general x1, matrix products, tile_products(): jnp.einsum('hqptsx,hptsy->shqxy', paired, col_tiles, preferred_element_ty...  4.65 us
    unnamed x6, local copies, waits for them, and re-layouts  1.03 us
    reshape x2, local copies, waits for them, and re-layouts, on_device(): spectra.transpose(3, 4, 2, 1, 0)  0.87 us
    reshape x1, local copies, waits for them, and re-layouts, on_device(): products = products.reshape(local_inputs, time_steps, TAPS, 2, channels)  0.75 us
  transfers between devices with their start and end apart: 1, of which 1 were waited for; matrix products, arithmetic and copies ran while one was open for 0% of the time, Pallas kernels for 0%

profile of v2, /device:TPU:0, one launch (start us, length us, event | category | flops | bytes accessed | tf_op | source)
XLA Modules:
  0.0 34.6 jit_solution(3851992101720079578)
XLA Ops:
  0.0 0.6 %fusion.22.refs_0_ = f32[4,4096]{1,0:T(4,128)S(1)} fusion(), kind=kLoop, calls=%fused_computation.40 | loop fusion | flops 720896 | bytes 65536 | tf_op jit(solution)/shard_map/div | solution.py:29
  0.6 0.6 %fusion.24 = (f32[64,512]{1,0:T(8,128)S(1)}, f32[64,512]{1,0:T(8,128)S(1)}) fusion(s32[64]{0:T(128)S(1)} %iota_add_fusion.2), kind=kLoop, calls=%fused_computation.42 | loop fusion | flops 458752 | bytes 262400 | tf_op jit(solution)/shard_map/cos | solution.py:37
  1.2 0.1 fusion.34
  1.3 0.1 pad_maximum_fusion.1
  1.5 0.2 broadcast_in_dim.13.refs_2_
  1.6 0.0 copy-start
  1.7 8.2 %shard_map.28 = f32[256,512]{1,0:T(8,128)S(1)} custom-call(f32[4,4096]{1,0:T(4,128)S(1)} %fusion.22.refs_0_, f32[128,512]{1,0:T(8,128)S(1)} %pad_maximum_fusion.refs_1_, f32[8,128,128]{2,1,0:T(8,128)S(1)} %broadcast_in_dim.13.refs_2_, s32[32,8,2,4096]{3,2,1,0:T(2,128)} %refs_3_.1), custom_call_target="tpu_custom_call" | custom-call | flops 2147483648 | bytes 9699328 | tf_op jit(solution)/shard_map/pallas_call | solution.py:111
  9.8 0.8 %reshape.56 = f32[32,8,4,2,64]{4,3,2,1,0:T(2,128)S(1)} reshape(f32[256,512]{1,0:T(8,128)S(1)} %shard_map.28) | data formatting | bytes 1048576 | tf_op jit(solution)/shard_map/reshape | solution.py:177
  10.6 0.1 slice.28
  10.7 0.1 slice.29
  10.7 0.1 slice.30
  10.8 0.1 slice.31
  10.9 0.3 copy.43
  11.2 0.3 copy.42
  11.5 0.3 copy.41
  11.7 0.3 copy.40
  12.0 0.3 fusion.3
  12.3 0.2 reshape.84
  12.5 0.7 %copy.31 = bf16[32,2,2,256]{3,2,1,0:T(2,128)(2,1)} copy(bf16[32,2,2,256]{3,1,0,2:T(2,128)(2,1)S(1)} %reshape.84) | data formatting | bytes 131072 | tf_op jit(solution)/shard_map/reshape | solution.py:192
  13.2 7.3 %all-to-all-start = ((bf16[32,2,2,256]{3,2,1,0:T(2,128)(2,1)}), bf16[32,2,2,256]{3,2,1,0:T(2,128)(2,1)S(1)}, u32[]{:S(2)}, u32[]{:S(2)}) async-start(bf16[32,2,2,256]{3,2,1,0:T(2,128)(2,1)} %copy.31), calls=%async_computation | async-start | bytes 131072 | tf_op jit(solution)/shard_map/all_to_all | solution.py:195
  20.5 0.0 copy-done
  20.5 0.1 convert_reduce_fusion
  20.6 7.2 %all-to-all-done = bf16[32,2,2,256]{3,2,1,0:T(2,128)(2,1)S(1)} async-done(((bf16[32,2,2,256]{3,2,1,0:T(2,128)(2,1)}), bf16[32,2,2,256]{3,2,1,0:T(2,128)(2,1)S(1)}, u32[]{:S(2)}, u32[]{:S(2)}) %all-to-all-start) | async-done | bytes 65568 | tf_op jit(solution)/shard_map/all_to_all | solution.py:195
  27.9 0.2 reshape.59
  28.1 0.1 copy.45
  28.2 0.2 reshape_reshape.3
  28.4 0.7 %gather_fusion.1 = bf16[36,2,2,8,128]{4,3,2,1,0:T(8,128)(2,1)S(1)} fusion(bf16[2,2,8,8,128]{4,2,3,1,0:T(8,128)(2,1)S(1)} %copy.33, s32[1024]{0:T(1024)S(1)} %pad_clamp_fusion), kind=kCustom, calls=%fused_computation.1.clone | custom fusion | bytes 589968 | tf_op jit(solution)/shard_map/jit(_take)/gather | solution.py:161
  29.0 0.7 %gather_fusion = bf16[36,2,2,8,128]{4,3,2,1,0:T(8,128)(2,1)S(1)} fusion(bf16[2,2,8,8,128]{4,2,3,1,0:T(8,128)(2,1)S(1)} %copy.33, s32[1024]{0:T(1024)S(1)} %pad_clamp_fusion.1), kind=kCustom, calls=%fused_computation.clone | custom fusion | bytes 589968 | tf_op jit(solution)/shard_map/jit(_take)/gather | solution.py:160
  29.7 0.1 fusion.14
  29.9 0.1 maximum_bitcast_fusion
  29.9 4.7 %bitcast_multiply_fusion = f32[36,2,2,128,128]{4,3,2,1,0:T(8,128)} fusion(bf16[2,1,2,8,36,128]{5,3,2,1,0,4:T(8,128)(2,1)S(1)} %maximum_bitcast_fusion, bf16[2,1,2,8,36,128]{5,3,2,1,0,4:T(8,128)(2,1)S(1)} %get-tuple-element.8, bf16[36,2,2,8,128]{4,3,2,1,0:T(8,128)(2,1)S(1)} %gather_fusion.1, pred[36]{0:T(512)(128)(4,1)S(1)} %get-tuple-element.6), kind=kOutput, calls=%fused_computation.2 | convolution fusion | flops 78299136 | bytes 10321956 | tf_op jit(solution)/shard_map/hqptsx,hptsy->shqxy/dot_general | solution.py:164
  (10 shorter events, 0.1 us)
Async XLA Ops:
  1.6 18.8 %copy-start = (s32[36]{0:T(128)S(1)}, s32[36]{0:T(128)}, u32[]{:S(2)}) copy-start(s32[36]{0:T(128)} %param.5) | copy-start | bytes 436
  13.2 14.7 %all-to-all-start = ((bf16[32,2,2,256]{3,2,1,0:T(2,128)(2,1)}), bf16[32,2,2,256]{3,2,1,0:T(2,128)(2,1)S(1)}, u32[]{:S(2)}, u32[]{:S(2)}) async-start(bf16[32,2,2,256]{3,2,1,0:T(2,128)(2,1)} %copy.31), calls=%async_computation | async-start | bytes 131072 | tf_op jit(solution)/shard_map/all_to_all | solution.py:195

commit v3 on v2

--- a/solution.py
+++ b/solution.py
@@ -41,7 +41,9 @@
     return first, jnp.broadcast_to(turn[:, :, None], turn.shape + (128,))
 
 
-def channelize_kernel(channels, proto_ref, first_ref, turn_ref, x_hbm, out_ref, buf, sems, acc_ref):
+def channelize_kernel(
+    channels, fold_shift, proto_ref, first_ref, turn_ref, x_hbm, out_ref, buf, sems, acc_ref
+):
     step = pl.program_id(0)
     count = pl.num_programs(0)
     cb = buf.shape[-1]
@@ -93,24 +95,42 @@
     def _():
         acc_ref[...] = part
 
-    @pl.when(step > 0)
+    @pl.when(jnp.logical_and(step > 0, step < count - 1))
     def _():
         acc_ref[...] += part
 
-    @pl.when(step == pl.num_programs(0) - 1)
-    def _():
-        out_ref[...] = acc_ref[...]
-
-
-def tap_products(voltages, proto, first, turn, channels):
+    @pl.when(step == count - 1)
+    def _():
+        products = acc_ref[...] + part
+        if not fold_shift:
+            out_ref[...] = products
+            return
+        time_steps = buf.shape[3]
+        width = 2 * channels
+        block = lax.broadcasted_iota(jnp.int32, (rows, width), 0) % time_steps
+        total = None
+        for tap in range(TAPS):
+            term = products[:, tap * width : (tap + 1) * width]
+            lead = TAPS - 1 - tap
+            if lead:
+                term = jnp.where(block >= lead, pltpu.roll(term, lead, 0), 0.0)
+            total = term if total is None else total + term
+        out_ref[...] = total.astype(out_ref.dtype)
+
+
+def tap_products(voltages, proto, first, turn, channels, fold_shift):
     local_inputs, time_steps = voltages.shape[0], voltages.shape[1]
     rows = local_inputs * time_steps
     width = TAPS * 2 * channels
     blocks = NCHAN // C_BLOCK
-    kernel = lambda *refs: channelize_kernel(channels, *refs)
+    kernel = lambda *refs: channelize_kernel(channels, fold_shift, *refs)
+    if fold_shift:
+        out_shape = jax.ShapeDtypeStruct((rows, 2 * channels), jnp.bfloat16)
+    else:
+        out_shape = jax.ShapeDtypeStruct((rows, width), jnp.float32)
     return pl.pallas_call(
         kernel,
-        out_shape=jax.ShapeDtypeStruct((rows, width), jnp.float32),
+        out_shape=out_shape,
         grid=(blocks,),
         in_specs=[
             pl.BlockSpec((TAPS, C_BLOCK), lambda j: (0, j)),
@@ -118,7 +138,7 @@
             pl.BlockSpec((None, 2 * channels, 128), lambda j: (j, 0, 0)),
             pl.BlockSpec(memory_space=pl.ANY),
         ],
-        out_specs=pl.BlockSpec((rows, width), lambda j: (0, 0)),
+        out_specs=pl.BlockSpec(out_shape.shape, lambda j: (0, 0)),
         scratch_shapes=[
             pltpu.VMEM((2, 2, local_inputs, time_steps, C_BLOCK), jnp.int32),
             pltpu.SemaphoreType.DMA((2, 2)),
@@ -173,21 +193,21 @@
     first_channel = NCHAN // 2 - channels // 2
     proto = prototype_rows()
     first, turn = phase_tables(first_channel, channels)
-    products = tap_products(voltages, proto, first, turn, channels)
-    products = products.reshape(local_inputs, time_steps, TAPS, 2, channels)
-    tail = products[:, time_steps - (TAPS - 1) :]
-    if time_devices > 1:
+    if time_devices == 1:
+        spectra = tap_products(voltages, proto, first, turn, channels, True)
+    else:
+        products = tap_products(voltages, proto, first, turn, channels, False)
+        products = products.reshape(local_inputs, time_steps, TAPS, 2, channels)
+        tail = products[:, time_steps - (TAPS - 1) :]
         previous = passed_along(tail, "tm", 1)
-    else:
-        previous = jnp.zeros_like(tail)
-    total = None
-    for tap in range(TAPS):
-        lead = TAPS - 1 - tap
-        shifted = jnp.concatenate(
-            [previous[:, tap:, tap], products[:, : time_steps - lead, tap]], axis=1
-        )
-        total = shifted if total is None else total + shifted
-    spectra = total.astype(jnp.bfloat16)
+        total = None
+        for tap in range(TAPS):
+            lead = TAPS - 1 - tap
+            shifted = jnp.concatenate(
+                [previous[:, tap:, tap], products[:, : time_steps - lead, tap]], axis=1
+            )
+            total = shifted if total is None else total + shifted
+        spectra = total.astype(jnp.bfloat16)
     spectra = spectra.reshape(local_inputs, time_steps, 2, freq_devices, CH_DEV)
     spectra = spectra.transpose(3, 4, 2, 1, 0).reshape(
         freq_devices, CH_DEV, 2, time_steps * local_inputs

time: 34.9 us -> 34.1 us (0.977)
  local copies, waits for them, and re-layouts: 4.95 us -> 4.5 us
    unnamed x6 -> x2, local copies, waits for them, and re-layouts: 1.03 us -> 0.01 us
    reshape x1, local copies, waits for them, and re-layouts: 0.75 us -> 1.2 us  [on_device(): spectra = spectra.reshape(local_inputs, time_steps, 2, freq_devices, CH_DEV)]
where the time goes in v3:
time: 34.1 us; the launch traced here: 33.8 us
  Pallas kernels  8.18 us (24%)
  starting transfers between devices  7.33 us (21%)
  waiting for transfers between devices  7.24 us (21%)
  matrix products  4.65 us (14%)
  local copies, waits for them, and re-layouts  4.5 us (13%)
  other arithmetic  1.77 us (5%)
    pallas_call x1, Pallas kernels, tap_products(): pl.pallas_call(kernel, out_shape=out_shape, grid=(blocks,), in_specs=[pl....  8.18 us
    all_to_all x1, starting transfers between devices, on_device(): lax.all_to_all(spectra, 'freq', split_axis=0, concat_axis=0, tiled=True)  7.33 us
    all_to_all x1, waiting for transfers between devices, on_device(): lax.all_to_all(spectra, 'freq', split_axis=0, concat_axis=0, tiled=True)  7.24 us
    dot_general x1, matrix products, tile_products(): jnp.einsum('hqptsx,hptsy->shqxy', paired, col_tiles, preferred_element_ty...  4.65 us
    reshape x2, local copies, waits for them, and re-layouts, on_device(): spectra.transpose(3, 4, 2, 1, 0)  1.21 us
    reshape x1, local copies, waits for them, and re-layouts, on_device(): spectra = spectra.reshape(local_inputs, time_steps, 2, freq_devices, CH_DEV)  1.2 us
  transfers between devices with their start and end apart: 1, of which 1 were waited for; matrix products, arithmetic and copies ran while one was open for 0% of the time, Pallas kernels for 0%

profile of v3, /device:TPU:0, one launch (start us, length us, event | category | flops | bytes accessed | tf_op | source)
XLA Modules:
  0.0 33.8 jit_solution(16358757478421318681)
XLA Ops:
  0.0 0.0 copy-start
  0.0 0.6 %fusion.21.refs_0_ = f32[4,4096]{1,0:T(4,128)S(1)} fusion(), kind=kLoop, calls=%fused_computation.38 | loop fusion | flops 720896 | bytes 65536 | tf_op jit(solution)/shard_map/div | solution.py:29
  0.6 0.6 %fusion.23 = (f32[64,512]{1,0:T(8,128)S(1)}, f32[64,512]{1,0:T(8,128)S(1)}) fusion(s32[64]{0:T(128)S(1)} %iota_add_fusion.2), kind=kLoop, calls=%fused_computation.40 | loop fusion | flops 458752 | bytes 262400 | tf_op jit(solution)/shard_map/cos | solution.py:37
  1.2 0.1 fusion.33
  1.4 0.1 pad_maximum_fusion.1
  1.5 0.2 broadcast_in_dim.13.refs_2_
  1.7 8.2 %shard_map.28 = bf16[256,128]{1,0:T(8,128)(2,1)S(1)} custom-call(f32[4,4096]{1,0:T(4,128)S(1)} %fusion.21.refs_0_, f32[128,512]{1,0:T(8,128)S(1)} %pad_maximum_fusion.refs_1_, f32[8,128,128]{2,1,0:T(8,128)S(1)} %broadcast_in_dim.13.refs_2_, s32[32,8,2,4096]{3,2,1,0:T(2,128)} %refs_3_.1), custom_call_target="tpu_custom_call" | custom-call | flops 2147483648 | bytes 9699328 | tf_op jit(solution)/shard_map/pallas_call | solution.py:131
  9.8 0.1 copy.17
  10.0 1.2 %reshape.53 = bf16[32,8,2,32,2]{1,0,4,3,2:T(8,128)(2,1)S(1)} reshape(bf16[256,128]{0,1:T(8,128)(2,1)S(1)} %copy.17) | data formatting | bytes 131072 | tf_op jit(solution)/shard_map/reshape | solution.py:211
  11.2 0.4 %copy.26 = bf16[32,2,2,8,32]{4,3,2,1,0:T(8,128)(2,1)S(1)} copy(bf16[32,2,2,8,32]{3,4,1,0,2:T(8,128)(2,1)S(1)} %bitcast.31) | data formatting | bytes 131072 | tf_op jit(solution)/shard_map/reshape | solution.py:212
  11.5 0.8 %reshape.80 = bf16[32,2,2,256]{3,2,1,0:T(2,128)(2,1)} reshape(bf16[32,2,2,8,32]{4,3,2,1,0:T(8,128)(2,1)S(1)} %copy.26) | data formatting | bytes 131072 | tf_op jit(solution)/shard_map/reshape | solution.py:212
  12.4 7.3 %all-to-all-start = ((bf16[32,2,2,256]{3,2,1,0:T(2,128)(2,1)}), bf16[32,2,2,256]{3,2,1,0:T(2,128)(2,1)S(1)}, u32[]{:S(2)}, u32[]{:S(2)}) async-start(bf16[32,2,2,256]{3,2,1,0:T(2,128)(2,1)} %reshape.80), calls=%async_computation | async-start | bytes 131072 | tf_op jit(solution)/shard_map/all_to_all | solution.py:215
  19.7 0.0 copy-done
  19.7 0.1 convert_reduce_fusion
  19.9 7.2 %all-to-all-done = bf16[32,2,2,256]{3,2,1,0:T(2,128)(2,1)S(1)} async-done(((bf16[32,2,2,256]{3,2,1,0:T(2,128)(2,1)}), bf16[32,2,2,256]{3,2,1,0:T(2,128)(2,1)S(1)}, u32[]{:S(2)}, u32[]{:S(2)}) %all-to-all-start) | async-done | bytes 65568 | tf_op jit(solution)/shard_map/all_to_all | solution.py:215
  27.1 0.2 reshape.55
  27.3 0.1 copy.29
  27.4 0.2 reshape_reshape.3
  27.6 0.7 %gather_fusion.1 = bf16[36,2,2,8,128]{4,3,2,1,0:T(8,128)(2,1)S(1)} fusion(bf16[2,2,8,8,128]{4,2,3,1,0:T(8,128)(2,1)S(1)} %copy.21, s32[1024]{0:T(1024)S(1)} %pad_clamp_fusion), kind=kCustom, calls=%fused_computation.1.clone | custom fusion | bytes 589968 | tf_op jit(solution)/shard_map/jit(_take)/gather | solution.py:181
  28.3 0.7 %gather_fusion = bf16[36,2,2,8,128]{4,3,2,1,0:T(8,128)(2,1)S(1)} fusion(bf16[2,2,8,8,128]{4,2,3,1,0:T(8,128)(2,1)S(1)} %copy.21, s32[1024]{0:T(1024)S(1)} %pad_clamp_fusion.1), kind=kCustom, calls=%fused_computation.clone | custom fusion | bytes 589968 | tf_op jit(solution)/shard_map/jit(_take)/gather | solution.py:180
  28.9 0.1 fusion.13
  29.1 0.1 maximum_bitcast_fusion
  29.2 4.7 %bitcast_multiply_fusion = f32[36,2,2,128,128]{4,3,2,1,0:T(8,128)} fusion(bf16[2,1,2,8,36,128]{5,3,2,1,0,4:T(8,128)(2,1)S(1)} %maximum_bitcast_fusion, bf16[2,1,2,8,36,128]{5,3,2,1,0,4:T(8,128)(2,1)S(1)} %get-tuple-element.8, bf16[36,2,2,8,128]{4,3,2,1,0:T(8,128)(2,1)S(1)} %gather_fusion.1, pred[36]{0:T(512)(128)(4,1)S(1)} %get-tuple-element.6), kind=kOutput, calls=%fused_computation.2 | convolution fusion | flops 78299136 | bytes 10321956 | tf_op jit(solution)/shard_map/hqptsx,hptsy->shqxy/dot_general | solution.py:184
  (10 shorter events, 0.1 us)
Async XLA Ops:
  0.0 19.7 %copy-start = (s32[36]{0:T(128)S(1)}, s32[36]{0:T(128)}, u32[]{:S(2)}) copy-start(s32[36]{0:T(128)} %param.5) | copy-start | bytes 436
  12.4 14.7 %all-to-all-start = ((bf16[32,2,2,256]{3,2,1,0:T(2,128)(2,1)}), bf16[32,2,2,256]{3,2,1,0:T(2,128)(2,1)S(1)}, u32[]{:S(2)}, u32[]{:S(2)}) async-start(bf16[32,2,2,256]{3,2,1,0:T(2,128)(2,1)} %reshape.80), calls=%async_computation | async-start | bytes 131072 | tf_op jit(solution)/shard_map/all_to_all | solution.py:215

commit v4 on v3

--- a/solution.py
+++ b/solution.py
@@ -34,11 +34,15 @@
     step = 2.0 * math.pi / NCHAN
     lane = jnp.arange(C_BLOCK, dtype=jnp.int32)
     start = ((lane[None, :] * channel[:, None]) % NCHAN).astype(jnp.float32) * step
-    first = jnp.concatenate([jnp.cos(start), jnp.sin(start)], axis=0)
+    cos_0, sin_0 = jnp.cos(start), jnp.sin(start)
+    even = jnp.stack([cos_0, -sin_0], axis=1).reshape(2 * channels, C_BLOCK)
+    odd = jnp.stack([sin_0, cos_0], axis=1).reshape(2 * channels, C_BLOCK)
     block = jnp.arange(NCHAN // C_BLOCK, dtype=jnp.int32) * C_BLOCK
     shift = ((block[:, None] * channel[None, :]) % NCHAN).astype(jnp.float32) * step
-    turn = jnp.concatenate([jnp.cos(shift), jnp.sin(shift)], axis=1)
-    return first, jnp.broadcast_to(turn[:, :, None], turn.shape + (128,))
+    cos_t = jnp.repeat(jnp.cos(shift), 2, axis=1)
+    sin_t = jnp.repeat(jnp.sin(shift), 2, axis=1)
+    turn = jnp.concatenate([cos_t, sin_t], axis=1)
+    return jnp.concatenate([even, odd], axis=0), jnp.broadcast_to(turn[:, :, None], turn.shape + (128,))
 
 
 def channelize_kernel(
@@ -68,12 +72,10 @@
             x_hbm.at[:, :, part, pl.ds(0, cb)], buf.at[slot, part], sems.at[slot, part]
         ).wait()
     turn = jnp.concatenate([turn_ref[...]] * (cb // turn_ref.shape[-1]), axis=1)
-    cos_0, sin_0 = first_ref[:channels], first_ref[channels:]
-    cos_t, sin_t = turn[:channels], turn[channels:]
-    cosine = cos_0 * cos_t - sin_0 * sin_t
-    sine = sin_0 * cos_t + cos_0 * sin_t
-    upper = jnp.concatenate([cosine, -sine], axis=0)
-    lower = jnp.concatenate([sine, cosine], axis=0)
+    even, odd = first_ref[: 2 * channels], first_ref[2 * channels :]
+    cos_t, sin_t = turn[: 2 * channels], turn[2 * channels :]
+    upper = even * cos_t - odd * sin_t
+    lower = odd * cos_t + even * sin_t
     weights = proto_ref[...]
     re_tables = []
     im_tables = []
@@ -115,7 +117,7 @@
             if lead:
                 term = jnp.where(block >= lead, pltpu.roll(term, lead, 0), 0.0)
             total = term if total is None else total + term
-        out_ref[...] = total.astype(out_ref.dtype)
+        out_ref[...] = total.T.astype(out_ref.dtype)
 
 
 def tap_products(voltages, proto, first, turn, channels, fold_shift):
@@ -125,7 +127,7 @@
     blocks = NCHAN // C_BLOCK
     kernel = lambda *refs: channelize_kernel(channels, fold_shift, *refs)
     if fold_shift:
-        out_shape = jax.ShapeDtypeStruct((rows, 2 * channels), jnp.bfloat16)
+        out_shape = jax.ShapeDtypeStruct((2 * channels, rows), jnp.bfloat16)
     else:
         out_shape = jax.ShapeDtypeStruct((rows, width), jnp.float32)
     return pl.pallas_call(
@@ -134,8 +136,8 @@
         grid=(blocks,),
         in_specs=[
             pl.BlockSpec((TAPS, C_BLOCK), lambda j: (0, j)),
-            pl.BlockSpec((2 * channels, C_BLOCK), lambda j: (0, 0)),
-            pl.BlockSpec((None, 2 * channels, 128), lambda j: (j, 0, 0)),
+            pl.BlockSpec((4 * channels, C_BLOCK), lambda j: (0, 0)),
+            pl.BlockSpec((None, 4 * channels, 128), lambda j: (j, 0, 0)),
             pl.BlockSpec(memory_space=pl.ANY),
         ],
         out_specs=pl.BlockSpec(out_shape.shape, lambda j: (0, 0)),
@@ -168,8 +170,8 @@
     freq_count = gathered.shape[1]
     local_chans = gathered.shape[2]
     inner_width = gathered.shape[4] // time_steps
-    unfolded = gathered.reshape(piece_count, freq_count, local_chans, 2, time_steps, inner_width)
-    unfolded = unfolded.transpose(2, 3, 0, 4, 1, 5)
+    unfolded = gathered.reshape(piece_count, freq_count, local_chans, 2, inner_width, time_steps)
+    unfolded = unfolded.transpose(2, 3, 0, 5, 1, 4)
     return unfolded.reshape(local_chans, 2, piece_count * time_steps, freq_count * inner_width)
 
 
@@ -197,7 +199,7 @@
         spectra = tap_products(voltages, proto, first, turn, channels, True)
     else:
         products = tap_products(voltages, proto, first, turn, channels, False)
-        products = products.reshape(local_inputs, time_steps, TAPS, 2, channels)
+        products = products.reshape(local_inputs, time_steps, TAPS, 2 * channels)
         tail = products[:, time_steps - (TAPS - 1) :]
         previous = passed_along(tail, "tm", 1)
         total = None
@@ -207,11 +209,8 @@
                 [previous[:, tap:, tap], products[:, : time_steps - lead, tap]], axis=1
             )
             total = shifted if total is None else total + shifted
-        spectra = total.astype(jnp.bfloat16)
-    spectra = spectra.reshape(local_inputs, time_steps, 2, freq_devices, CH_DEV)
-    spectra = spectra.transpose(3, 4, 2, 1, 0).reshape(
-        freq_devices, CH_DEV, 2, time_steps * local_inputs
-    )
+        spectra = total.astype(jnp.bfloat16).reshape(local_inputs * time_steps, 2 * channels).T
+    spectra = spectra.reshape(freq_devices, CH_DEV, 2, local_inputs * time_steps)
     turned = lax.all_to_all(spectra, "freq", split_axis=0, concat_axis=0, tiled=True)
     slot_count = tile_map.shape[0] // time_devices
     inverse_count = 1.0 / (time_steps * time_devices)

time: 34.1 us -> 33.9 us (level)
  local copies, waits for them, and re-layouts: 4.5 us -> 4.02 us
    reshape x5, local copies, waits for them, and re-layouts: 2.69 us -> 1.12 us  [the longest x1 0.66 us: on_device(): spectra.reshape(freq_devices, CH_DEV, 2, local_inputs * time_steps)]
    neg x0 -> x1, other arithmetic: none -> 0.6 us  [phase_tables(): even = jnp.stack([cos_0, -sin_0], axis=1).reshape(2 * channels, C_BLOCK)]
    cos x2 -> x1, other arithmetic: 0.71 us -> 0.12 us  [phase_tables(): cos_t = jnp.repeat(jnp.cos(shift), 2, axis=1)]
    another operation x0 -> x2, local copies, waits for them, and re-layouts: none -> 0.41 us  [the longest x1 0.2 us: phase_tables(): even = jnp.stack([cos_0, -sin_0], axis=1).reshape(2 * channels, C_BLOCK)]
where the time goes in v4:
time: 33.9 us; the launch traced here: 33.6 us
  Pallas kernels  8.37 us (25%)
  starting transfers between devices  7.33 us (22%)
  waiting for transfers between devices  7.24 us (21%)
  matrix products  4.65 us (14%)
  local copies, waits for them, and re-layouts  4.02 us (12%)
  other arithmetic  1.77 us (5%)
    pallas_call x1, Pallas kernels, tap_products(): pl.pallas_call(kernel, out_shape=out_shape, grid=(blocks,), in_specs=[pl....  8.37 us
    all_to_all x1, starting transfers between devices, on_device(): lax.all_to_all(spectra, 'freq', split_axis=0, concat_axis=0, tiled=True)  7.33 us
    all_to_all x1, waiting for transfers between devices, on_device(): lax.all_to_all(spectra, 'freq', split_axis=0, concat_axis=0, tiled=True)  7.24 us
    dot_general x1, matrix products, tile_products(): jnp.einsum('hqptsx,hptsy->shqxy', paired, col_tiles, preferred_element_ty...  4.65 us
  transfers between devices with their start and end apart: 1, of which 1 were waited for; matrix products, arithmetic and copies ran while one was open for 0% of the time, Pallas kernels for 0%

profile of v4, /device:TPU:0, one launch (start us, length us, event | category | flops | bytes accessed | tf_op | source)
XLA Modules:
  0.0 33.6 jit_solution(15696502296944154989)
XLA Ops:
  0.0 0.0 copy-start
  0.0 0.6 %fusion.21.refs_0_ = f32[4,4096]{1,0:T(4,128)S(1)} fusion(), kind=kLoop, calls=%fused_computation.39 | loop fusion | flops 720896 | bytes 65536 | tf_op jit(solution)/shard_map/div | solution.py:29
  0.6 0.6 %fusion.29 = (f32[64,1,512]{2,0,1:T(8,128)S(1)}, f32[64,1,512]{2,0,1:T(8,128)S(1)}, f32[64,1,512]{2,0,1:T(8,128)S(1)}) fusion(s32[64]{0:T(128)S(1)} %iota_add_fusion.2), kind=kLoop, calls=%fused_computation.53 | loop fusion | flops 491520 | bytes 393472 | tf_op jit(solution)/shard_map/neg | solution.py:38
  1.2 0.1 fusion.34
  1.4 0.1 copy.26
  1.5 0.1 copy.27
  1.7 0.1 pad_maximum_fusion.1
  1.8 0.2 copy.24
  2.0 0.2 reshape.179
  2.2 0.2 copy.25
  2.4 0.2 reshape.180
  2.6 0.3 broadcast_in_dim.35.refs_2_
  3.0 8.4 %shard_map.28 = bf16[128,256]{1,0:T(8,128)(2,1)S(1)} custom-call(f32[4,4096]{1,0:T(4,128)S(1)} %fusion.21.refs_0_, f32[256,512]{1,0:T(8,128)S(1)} %pad_maximum_fusion.refs_1_, f32[8,256,128]{2,1,0:T(8,128)S(1)} %broadcast_in_dim.35.refs_2_, s32[32,8,2,4096]{3,2,1,0:T(2,128)} %refs_3_.1), custom_call_target="tpu_custom_call" | custom-call | flops 2147483648 | bytes 10485760 | tf_op jit(solution)/shard_map/pallas_call | solution.py:133
  11.3 0.7 %reshape.183 = bf16[32,2,2,256]{3,2,1,0:T(2,128)(2,1)} reshape(bf16[128,256]{1,0:T(8,128)(2,1)S(1)} %shard_map.28) | data formatting | bytes 131072 | tf_op jit(solution)/shard_map/reshape | solution.py:213
  12.0 7.3 %all-to-all-start = ((bf16[32,2,2,256]{3,2,1,0:T(2,128)(2,1)}), bf16[32,2,2,256]{3,2,1,0:T(2,128)(2,1)S(1)}, u32[]{:S(2)}, u32[]{:S(2)}) async-start(bf16[32,2,2,256]{3,2,1,0:T(2,128)(2,1)} %reshape.183), calls=%async_computation | async-start | bytes 131072 | tf_op jit(solution)/shard_map/all_to_all | solution.py:214
  19.4 0.0 copy-done
  19.4 0.1 convert_reduce_fusion
  19.5 7.2 %all-to-all-done = bf16[32,2,2,256]{3,2,1,0:T(2,128)(2,1)S(1)} async-done(((bf16[32,2,2,256]{3,2,1,0:T(2,128)(2,1)}), bf16[32,2,2,256]{3,2,1,0:T(2,128)(2,1)S(1)}, u32[]{:S(2)}, u32[]{:S(2)}) %all-to-all-start) | async-done | bytes 65568 | tf_op jit(solution)/shard_map/all_to_all | solution.py:214
  26.7 0.2 copy.30
  26.9 0.2 copy.31
  27.2 0.2 reshape_reshape.3
  27.4 0.7 %gather_fusion.1 = bf16[36,2,2,8,128]{4,3,2,1,0:T(8,128)(2,1)S(1)} fusion(bf16[2,2,8,8,128]{4,2,3,1,0:T(8,128)(2,1)S(1)} %copy.32, s32[1024]{0:T(1024)S(1)} %pad_clamp_fusion), kind=kCustom, calls=%fused_computation.1.clone | custom fusion | bytes 589968 | tf_op jit(solution)/shard_map/jit(_take)/gather | solution.py:183
  28.0 0.7 %gather_fusion = bf16[36,2,2,8,128]{4,3,2,1,0:T(8,128)(2,1)S(1)} fusion(bf16[2,2,8,8,128]{4,2,3,1,0:T(8,128)(2,1)S(1)} %copy.32, s32[1024]{0:T(1024)S(1)} %pad_clamp_fusion.1), kind=kCustom, calls=%fused_computation.clone | custom fusion | bytes 589968 | tf_op jit(solution)/shard_map/jit(_take)/gather | solution.py:182
  28.7 0.1 fusion.13
  28.9 0.1 maximum_bitcast_fusion
  28.9 4.7 %bitcast_multiply_fusion = f32[36,2,2,128,128]{4,3,2,1,0:T(8,128)} fusion(bf16[2,1,2,8,36,128]{5,3,2,1,0,4:T(8,128)(2,1)S(1)} %maximum_bitcast_fusion, bf16[2,1,2,8,36,128]{5,3,2,1,0,4:T(8,128)(2,1)S(1)} %get-tuple-element.8, bf16[36,2,2,8,128]{4,3,2,1,0:T(8,128)(2,1)S(1)} %gather_fusion.1, pred[36]{0:T(512)(128)(4,1)S(1)} %get-tuple-element.6), kind=kOutput, calls=%fused_computation.2 | convolution fusion | flops 78299136 | bytes 10321956 | tf_op jit(solution)/shard_map/hqptsx,hptsy->shqxy/dot_general | solution.py:186
  (15 shorter events, 0.3 us)
Async XLA Ops:
  0.0 19.4 %copy-start = (s32[36]{0:T(128)S(1)}, s32[36]{0:T(128)}, u32[]{:S(2)}) copy-start(s32[36]{0:T(128)} %param.5) | copy-start | bytes 436
  12.0 14.7 %all-to-all-start = ((bf16[32,2,2,256]{3,2,1,0:T(2,128)(2,1)}), bf16[32,2,2,256]{3,2,1,0:T(2,128)(2,1)S(1)}, u32[]{:S(2)}, u32[]{:S(2)}) async-start(bf16[32,2,2,256]{3,2,1,0:T(2,128)(2,1)} %reshape.183), calls=%async_computation | async-start | bytes 131072 | tf_op jit(solution)/shard_map/all_to_all | solution.py:214

commit v5 on v4

--- a/solution.py
+++ b/solution.py
@@ -30,19 +30,22 @@
 
 
 def phase_tables(first_channel, channels):
-    channel = first_channel + jnp.arange(channels, dtype=jnp.int32)
+    rows = 4 * channels
     step = 2.0 * math.pi / NCHAN
-    lane = jnp.arange(C_BLOCK, dtype=jnp.int32)
-    start = ((lane[None, :] * channel[:, None]) % NCHAN).astype(jnp.float32) * step
-    cos_0, sin_0 = jnp.cos(start), jnp.sin(start)
-    even = jnp.stack([cos_0, -sin_0], axis=1).reshape(2 * channels, C_BLOCK)
-    odd = jnp.stack([sin_0, cos_0], axis=1).reshape(2 * channels, C_BLOCK)
-    block = jnp.arange(NCHAN // C_BLOCK, dtype=jnp.int32) * C_BLOCK
-    shift = ((block[:, None] * channel[None, :]) % NCHAN).astype(jnp.float32) * step
-    cos_t = jnp.repeat(jnp.cos(shift), 2, axis=1)
-    sin_t = jnp.repeat(jnp.sin(shift), 2, axis=1)
-    turn = jnp.concatenate([cos_t, sin_t], axis=1)
-    return jnp.concatenate([even, odd], axis=0), jnp.broadcast_to(turn[:, :, None], turn.shape + (128,))
+    quarter = NCHAN // 4
+    row = lax.broadcasted_iota(jnp.int32, (rows, C_BLOCK), 0)
+    lane = lax.broadcasted_iota(jnp.int32, (rows, C_BLOCK), 1)
+    channel = first_channel + (row % (2 * channels)) // 2
+    part = row % 2
+    offset = jnp.where(row >= 2 * channels, (1 - part) * 3 * quarter, part * quarter)
+    first = jnp.cos(((lane * channel + offset) % NCHAN).astype(jnp.float32) * step)
+    blocks = NCHAN // C_BLOCK
+    block = lax.broadcasted_iota(jnp.int32, (blocks, rows), 0) * C_BLOCK
+    row = lax.broadcasted_iota(jnp.int32, (blocks, rows), 1)
+    channel = first_channel + (row % (2 * channels)) // 2
+    offset = jnp.where(row >= 2 * channels, 3 * quarter, 0)
+    turn = jnp.cos(((block * channel + offset) % NCHAN).astype(jnp.float32) * step)
+    return first, jnp.broadcast_to(turn[:, :, None], (blocks, rows, 128))
 
 
 def channelize_kernel(

time: 33.9 us -> 35.5 us (1.047)
  other arithmetic: 1.77 us -> 4.59 us
  local copies, waits for them, and re-layouts: 4.02 us -> 2.92 us
    cos x1 -> x2, other arithmetic: 0.12 us -> 3.61 us  [the longest x1 3.49 us: phase_tables(): jnp.cos(((lane * channel + offset) % NCHAN).astype(jnp.float32) * step)]
    neg x1 -> x0, other arithmetic: 0.6 us -> none  [phase_tables(): even = jnp.stack([cos_0, -sin_0], axis=1).reshape(2 * channels, C_BLOCK)]
    reshape x4 -> x0, local copies, waits for them, and re-layouts: 0.46 us -> none  [the longest x1 0.18 us: phase_tables(): even = jnp.stack([cos_0, -sin_0], axis=1).reshape(2 * channels, C_BLOCK)]
    another operation x2 -> x0, local copies, waits for them, and re-layouts: 0.41 us -> none  [the longest x1 0.2 us: phase_tables(): even = jnp.stack([cos_0, -sin_0], axis=1).reshape(2 * channels, C_BLOCK)]
where the time goes in v5:
time: 35.5 us; the launch traced here: 35.3 us
  Pallas kernels  8.38 us (24%)
  starting transfers between devices  7.33 us (21%)
  waiting for transfers between devices  7.24 us (20%)
  matrix products  4.65 us (13%)
  other arithmetic  4.59 us (13%)
  local copies, waits for them, and re-layouts  2.92 us (8%)
    pallas_call x1, Pallas kernels, tap_products(): pl.pallas_call(kernel, out_shape=out_shape, grid=(blocks,), in_specs=[pl....  8.38 us
    all_to_all x1, starting transfers between devices, on_device(): lax.all_to_all(spectra, 'freq', split_axis=0, concat_axis=0, tiled=True)  7.33 us
    all_to_all x1, waiting for transfers between devices, on_device(): lax.all_to_all(spectra, 'freq', split_axis=0, concat_axis=0, tiled=True)  7.24 us
    dot_general x1, matrix products, tile_products(): jnp.einsum('hqptsx,hptsy->shqxy', paired, col_tiles, preferred_element_ty...  4.65 us
    cos x1, other arithmetic, phase_tables(): jnp.cos(((lane * channel + offset) % NCHAN).astype(jnp.float32) * step)  3.49 us
  transfers between devices with their start and end apart: 1, of which 1 were waited for; matrix products, arithmetic and copies ran while one was open for 0% of the time, Pallas kernels for 0%

profile of v5, /device:TPU:0, one launch (start us, length us, event | category | flops | bytes accessed | tf_op | source)
XLA Modules:
  0.0 35.3 jit_solution(3463243332617122069)
XLA Ops:
  0.0 0.0 copy-start
  0.0 0.6 %fusion.29.refs_0_ = f32[4,4096]{1,0:T(4,128)S(1)} fusion(), kind=kLoop, calls=%fused_computation.53 | loop fusion | flops 720896 | bytes 65536 | tf_op jit(solution)/shard_map/div | solution.py:29
  0.7 0.1 fusion.42
  0.8 3.5 %fusion.12.refs_1_ = f32[256,512]{1,0:T(8,128)S(1)} fusion(s32[256]{0:T(256)S(1)} %get-tuple-element.13, s32[256]{0:T(256)S(1)} %get-tuple-element.18, s32[256]{0:T(256)S(1)} %get-tuple-element.14, s32[256]{0:T(256)S(1)} %get-tuple-element.17, pred[256]{0:T(512)(128)(4,1)S(1)} %get-tuple-element.16, pred[256]{0:T(512)(128)(4,1)S(1)} %get-tuple-element.15, ...), kind=kLoop, calls=%fused_computation.27 | loop fusion | flops 4849664 | bytes 529152 | tf_op jit(solution)/shard_map/cos | solution.py:41
  4.3 0.3 broadcast_in_dim.30.refs_2_
  4.6 8.4 %shard_map.28 = bf16[128,256]{1,0:T(8,128)(2,1)S(1)} custom-call(f32[4,4096]{1,0:T(4,128)S(1)} %fusion.29.refs_0_, f32[256,512]{1,0:T(8,128)S(1)} %fusion.12.refs_1_, f32[8,256,128]{2,1,0:T(8,128)S(1)} %broadcast_in_dim.30.refs_2_, s32[32,8,2,4096]{3,2,1,0:T(2,128)} %refs_3_.1), custom_call_target="tpu_custom_call" | custom-call | flops 2147483648 | bytes 10485760 | tf_op jit(solution)/shard_map/pallas_call | solution.py:136
  13.0 0.7 %reshape.123 = bf16[32,2,2,256]{3,2,1,0:T(2,128)(2,1)} reshape(bf16[128,256]{1,0:T(8,128)(2,1)S(1)} %shard_map.28) | data formatting | bytes 131072 | tf_op jit(solution)/shard_map/reshape | solution.py:216
  13.7 7.3 %all-to-all-start = ((bf16[32,2,2,256]{3,2,1,0:T(2,128)(2,1)}), bf16[32,2,2,256]{3,2,1,0:T(2,128)(2,1)S(1)}, u32[]{:S(2)}, u32[]{:S(2)}) async-start(bf16[32,2,2,256]{3,2,1,0:T(2,128)(2,1)} %reshape.123), calls=%async_computation | async-start | bytes 131072 | tf_op jit(solution)/shard_map/all_to_all | solution.py:217
  21.0 0.0 copy-done
  21.0 0.1 convert_reduce_fusion
  21.2 7.2 %all-to-all-done = bf16[32,2,2,256]{3,2,1,0:T(2,128)(2,1)S(1)} async-done(((bf16[32,2,2,256]{3,2,1,0:T(2,128)(2,1)}), bf16[32,2,2,256]{3,2,1,0:T(2,128)(2,1)S(1)}, u32[]{:S(2)}, u32[]{:S(2)}) %all-to-all-start) | async-done | bytes 65568 | tf_op jit(solution)/shard_map/all_to_all | solution.py:217
  28.4 0.2 copy.14
  28.6 0.2 copy.15
  28.9 0.2 reshape_reshape.3
  29.0 0.7 %gather_fusion.1 = bf16[36,2,2,8,128]{4,3,2,1,0:T(8,128)(2,1)S(1)} fusion(bf16[2,2,8,8,128]{4,2,3,1,0:T(8,128)(2,1)S(1)} %copy.16, s32[1024]{0:T(1024)S(1)} %pad_clamp_fusion), kind=kCustom, calls=%fused_computation.1.clone | custom fusion | bytes 589968 | tf_op jit(solution)/shard_map/jit(_take)/gather | solution.py:186
  29.7 0.7 %gather_fusion = bf16[36,2,2,8,128]{4,3,2,1,0:T(8,128)(2,1)S(1)} fusion(bf16[2,2,8,8,128]{4,2,3,1,0:T(8,128)(2,1)S(1)} %copy.16, s32[1024]{0:T(1024)S(1)} %pad_clamp_fusion.1), kind=kCustom, calls=%fused_computation.clone | custom fusion | bytes 589968 | tf_op jit(solution)/shard_map/jit(_take)/gather | solution.py:185
  30.4 0.1 fusion.21
  30.5 0.1 maximum_bitcast_fusion
  30.6 4.7 %bitcast_multiply_fusion = f32[36,2,2,128,128]{4,3,2,1,0:T(8,128)} fusion(bf16[2,1,2,8,36,128]{5,3,2,1,0,4:T(8,128)(2,1)S(1)} %maximum_bitcast_fusion, bf16[2,1,2,8,36,128]{5,3,2,1,0,4:T(8,128)(2,1)S(1)} %get-tuple-element.8, bf16[36,2,2,8,128]{4,3,2,1,0:T(8,128)(2,1)S(1)} %gather_fusion.1, pred[36]{0:T(512)(128)(4,1)S(1)} %get-tuple-element.6), kind=kOutput, calls=%fused_computation.2 | convolution fusion | flops 78299136 | bytes 10321956 | tf_op jit(solution)/shard_map/hqptsx,hptsy->shqxy/dot_general | solution.py:189
  (13 shorter events, 0.1 us)
Async XLA Ops:
  0.0 21.0 %copy-start = (s32[36]{0:T(128)S(1)}, s32[36]{0:T(128)}, u32[]{:S(2)}) copy-start(s32[36]{0:T(128)} %param.5) | copy-start | bytes 436
  13.7 14.7 %all-to-all-start = ((bf16[32,2,2,256]{3,2,1,0:T(2,128)(2,1)}), bf16[32,2,2,256]{3,2,1,0:T(2,128)(2,1)S(1)}, u32[]{:S(2)}, u32[]{:S(2)}) async-start(bf16[32,2,2,256]{3,2,1,0:T(2,128)(2,1)} %reshape.123), calls=%async_computation | async-start | bytes 131072 | tf_op jit(solution)/shard_map/all_to_all | solution.py:217

commit v6 on v4

--- a/solution.py
+++ b/solution.py
@@ -175,15 +175,56 @@
     return unfolded.reshape(local_chans, 2, piece_count * time_steps, freq_count * inner_width)
 
 
-def tile_products(spectra, tile_ids):
-    blocks = spectra.shape[3] // TB
-    row_block, col_block = tile_coords(tile_ids, blocks)
-    shaped = spectra.reshape(spectra.shape[0], 2, spectra.shape[2], blocks, TB)
-    row_tiles = jnp.take(shaped, row_block, axis=3)
-    col_tiles = jnp.take(shaped, col_block, axis=3)
-    turned = jnp.stack([row_tiles[:, 1], -row_tiles[:, 0]], axis=1)
-    paired = jnp.stack([row_tiles, turned], axis=1)
-    return jnp.einsum("hqptsx,hptsy->shqxy", paired, col_tiles, preferred_element_type=jnp.float32)
+def correlate_kernel(blocks, tiles_per_step, scale, ids_ref, lhs_ref, rhs_ref, out_ref):
+    step = pl.program_id(0)
+    for slot in range(tiles_per_step):
+        tile_id = ids_ref[step * tiles_per_step + slot]
+        row_block = jnp.int32(0)
+        for r in range(1, blocks):
+            row_block = row_block + (tile_id >= r * (r + 1) // 2).astype(jnp.int32)
+        col_block = tile_id - row_block * (row_block + 1) // 2
+        rows = pl.ds(pl.multiple_of(row_block * TB, TB), TB)
+        cols = pl.ds(pl.multiple_of(col_block * TB, TB), TB)
+        for chan in range(lhs_ref.shape[0]):
+            right = rhs_ref[chan, :, cols]
+            for part in range(2):
+                left = lhs_ref[chan, part, rows, :]
+                product = jnp.dot(left, right, preferred_element_type=jnp.float32)
+                out_ref[slot, chan, part] = product * scale
+
+
+def tile_products(spectra, tile_ids, scale):
+    local_chans, depth, paths = spectra.shape
+    blocks = paths // TB
+    half = depth // 2
+    turned_rows = spectra.transpose(0, 2, 1)
+    rotated = jnp.concatenate([turned_rows[:, :, half:], -turned_rows[:, :, :half]], axis=2)
+    lhs = jnp.stack([turned_rows, rotated], axis=1)
+    count = tile_ids.shape[0]
+    tiles_per_step = max(d for d in range(1, 10) if count % d == 0)
+    kernel = lambda *refs: correlate_kernel(blocks, tiles_per_step, scale, *refs)
+    out_block = (tiles_per_step, local_chans, 2, TB, TB)
+    return pl.pallas_call(
+        kernel,
+        out_shape=jax.ShapeDtypeStruct((count, local_chans, 2, TB, TB), jnp.float32),
+        grid_spec=pltpu.PrefetchScalarGridSpec(
+            num_scalar_prefetch=1,
+            grid=(count // tiles_per_step,),
+            in_specs=[
+                pl.BlockSpec(lhs.shape, lambda j, ids: (0, 0, 0, 0)),
+                pl.BlockSpec(spectra.shape, lambda j, ids: (0, 0, 0)),
+            ],
+            out_specs=pl.BlockSpec(out_block, lambda j, ids: (j, 0, 0, 0, 0)),
+        ),
+        compiler_params=pltpu.CompilerParams(
+            dimension_semantics=("arbitrary",), vmem_limit_bytes=48 * 1024 * 1024
+        ),
+        cost_estimate=pl.CostEstimate(
+            flops=2 * count * local_chans * 2 * TB * TB * depth,
+            transcendentals=0,
+            bytes_accessed=count * local_chans * 2 * TB * TB * 4 + lhs.size * 2 + spectra.size * 2,
+        ),
+    )(tile_ids, lhs, spectra)
 
 
 def on_device(voltages, tile_map):
@@ -215,10 +256,9 @@
     slot_count = tile_map.shape[0] // time_devices
     inverse_count = 1.0 / (time_steps * time_devices)
     tile_ids = lax.dynamic_slice_in_dim(tile_map, lax.axis_index("tm") * slot_count, slot_count)
-    summed = tile_products(
-        arrange_rows(lax.all_gather(turned[None], "tm", axis=0, tiled=True), time_steps), tile_ids
-    )
-    return summed * inverse_count
+    arranged = arrange_rows(lax.all_gather(turned[None], "tm", axis=0, tiled=True), time_steps)
+    arranged = arranged.reshape(arranged.shape[0], -1, arranged.shape[3])
+    return tile_products(arranged, tile_ids, inverse_count)
 
 
 def solution(mesh):

time: 33.9 us -> 32.5 us (0.959)
  blocking collectives: 0 us -> 14.5 us
  starting transfers between devices: 7.33 us -> 0 us
  waiting for transfers between devices: 7.24 us -> 0 us
  Pallas kernels: 8.37 us -> 13.4 us
  matrix products: 4.65 us -> 0 us
  local copies, waits for them, and re-layouts: 4.02 us -> 2.64 us
    all_to_all x0 -> x1, blocking collectives: none -> 14.5 us  [on_device(): lax.all_to_all(spectra, 'freq', split_axis=0, concat_axis=0, tiled=True)]
    all_to_all x1 -> x0, starting transfers between devices: 7.33 us -> none  [on_device(): lax.all_to_all(spectra, 'freq', split_axis=0, concat_axis=0, tiled=True)]
    all_to_all x1 -> x0, waiting for transfers between devices: 7.24 us -> none  [on_device(): lax.all_to_all(spectra, 'freq', split_axis=0, concat_axis=0, tiled=True)]
    pallas_call x0 -> x1, Pallas kernels: none -> 5.06 us  [tile_products(): pl.pallas_call(kernel, out_shape=jax.ShapeDtypeStruct((count, local_chans...]
    dot_general x1 -> x0, matrix products: 4.65 us -> none  [tile_products(): jnp.einsum('hqptsx,hptsy->shqxy', paired, col_tiles, preferred_element_ty...]
    gather x2 -> x0, local copies, waits for them, and re-layouts: 1.32 us -> none  [the longest x1 0.66 us: tile_products(): row_tiles = jnp.take(shaped, row_block, axis=3)]
    reshape x1, local copies, waits for them, and re-layouts: 0.66 us -> 0.03 us  [on_device(): spectra.reshape(freq_devices, CH_DEV, 2, local_inputs * time_steps)]
    another operation x2, local copies, waits for them, and re-layouts: 0.18 us -> 0.75 us  [the longest x1 0.47 us: tile_products(): lhs = jnp.stack([turned_rows, rotated], axis=1)]
  transfers between devices with their start and end apart: 1 -> 0, of which waited for: 1 -> 0; matrix products, arithmetic and copies ran while one was open for 0% -> 0% of each run, Pallas kernels for 0% -> 0%
where the time goes in v6:
time: 32.5 us; the launch traced here: 32.3 us
  blocking collectives  14.5 us (45%)
  Pallas kernels  13.4 us (41%)
  local copies, waits for them, and re-layouts  2.64 us (8%)
  other arithmetic  1.48 us (5%)
    all_to_all x1, blocking collectives, on_device(): lax.all_to_all(spectra, 'freq', split_axis=0, concat_axis=0, tiled=True)  14.5 us
    pallas_call x1, Pallas kernels, tap_products(): pl.pallas_call(kernel, out_shape=out_shape, grid=(blocks,), in_specs=[pl....  8.37 us
    pallas_call x1, Pallas kernels, tile_products(): pl.pallas_call(kernel, out_shape=jax.ShapeDtypeStruct((count, local_chans...  5.06 us

profile of v6, /device:TPU:0, one launch (start us, length us, event | category | flops | bytes accessed | tf_op | source)
XLA Modules:
  0.0 32.3 jit_solution(4093331929938622986)
XLA Ops:
  0.0 0.6 %fusion.12.refs_0_ = f32[4,4096]{1,0:T(4,128)S(1)} fusion(), kind=kLoop, calls=%fused_computation.25 | loop fusion | flops 720896 | bytes 65536 | tf_op jit(solution)/shard_map/div | solution.py:29
  0.6 0.6 %fusion.20 = (f32[64,1,512]{2,0,1:T(8,128)S(1)}, f32[64,1,512]{2,0,1:T(8,128)S(1)}, f32[64,1,512]{2,0,1:T(8,128)S(1)}) fusion(s32[64]{0:T(128)S(1)} %iota_add_fusion), kind=kLoop, calls=%fused_computation.40 | loop fusion | flops 491520 | bytes 393472 | tf_op jit(solution)/shard_map/neg | solution.py:38
  1.2 0.0 copy-start
  1.2 0.1 fusion.25
  1.4 0.1 copy.15
  1.5 0.1 copy.16
  1.7 0.1 pad_maximum_fusion.1
  1.8 0.2 copy.13
  2.0 0.2 reshape.151
  2.2 0.2 copy.14
  2.4 0.2 reshape.152
  2.7 0.3 %broadcast_in_dim.24.refs_2_ = f32[8,256,128]{2,1,0:T(8,128)S(1)} broadcast(f32[8,256]{1,0:T(8,128)S(1)} %pad_maximum_fusion.4), dimensions={0,1} | broadcast | bytes 1056768 | tf_op jit(solution)/shard_map/broadcast_in_dim | solution.py:45
  3.0 8.4 %shard_map.28 = bf16[128,256]{1,0:T(8,128)(2,1)S(1)} custom-call(f32[4,4096]{1,0:T(4,128)S(1)} %fusion.12.refs_0_, f32[256,512]{1,0:T(8,128)S(1)} %pad_maximum_fusion.refs_1_, f32[8,256,128]{2,1,0:T(8,128)S(1)} %broadcast_in_dim.24.refs_2_, s32[32,8,2,4096]{3,2,1,0:T(2,128)} %refs_3_.1), custom_call_target="tpu_custom_call" | custom-call | flops 2147483648 | bytes 10485760 | tf_op jit(solution)/shard_map/pallas_call | solution.py:133
  11.4 14.5 %all_to_all.5 = bf16[32,2,2,256]{3,2,1,0:T(2,128)(2,1)S(1)} all-to-all(bf16[32,2,2,256]{3,2,1,0:T(2,128)(2,1)S(1)} %reshape.155), channel_id=1, replica_groups=mesh['freq'=32,'tm'=1] {'freq'}, dimensions={0} | all-to-all | bytes 131072 | tf_op jit(solution)/shard_map/all_to_all | solution.py:255
  25.9 0.2 copy.19
  26.1 0.2 copy.20
  26.4 0.3 reshape_reshape.3.refs_2_
  26.7 0.5 %copy.21.refs_1_ = bf16[2,2,1024,16]{3,2,1,0:T(8,128)(2,1)S(1)} copy(bf16[2,2,1024,16]{2,3,0,1:T(8,128)(2,1)S(1)} %pad_maximum_fusion.3) | data formatting | bytes 262144 | tf_op jit(solution)/shard_map/stack | solution.py:202
  27.2 0.0 copy-done
  27.2 5.1 %shard_map.29 = f32[36,2,2,128,128]{4,3,2,1,0:T(8,128)} custom-call(s32[36]{0:T(128)S(1)} %copy-done, bf16[2,2,1024,16]{3,2,1,0:T(8,128)(2,1)S(1)} %copy.21.refs_1_, bf16[2,16,1024]{2,1,0:T(8,128)(2,1)S(1)} %reshape_reshape.3.refs_2_), custom_call_target="tpu_custom_call" | custom-call | flops 75497472 | bytes 9633792 | tf_op jit(solution)/shard_map/pallas_call | solution.py:207
  (12 shorter events, 0.3 us)
Async XLA Ops:
  1.2 25.9 %copy-start = (s32[36]{0:T(128)S(1)}, s32[36]{0:T(128)}, u32[]{:S(2)}) copy-start(s32[36]{0:T(128)} %refs_0_) | copy-start | bytes 436

commit v7 on v6

--- a/solution.py
+++ b/solution.py
@@ -34,19 +34,15 @@
     step = 2.0 * math.pi / NCHAN
     lane = jnp.arange(C_BLOCK, dtype=jnp.int32)
     start = ((lane[None, :] * channel[:, None]) % NCHAN).astype(jnp.float32) * step
-    cos_0, sin_0 = jnp.cos(start), jnp.sin(start)
-    even = jnp.stack([cos_0, -sin_0], axis=1).reshape(2 * channels, C_BLOCK)
-    odd = jnp.stack([sin_0, cos_0], axis=1).reshape(2 * channels, C_BLOCK)
+    first = jnp.concatenate([jnp.cos(start), jnp.sin(start)], axis=0)
     block = jnp.arange(NCHAN // C_BLOCK, dtype=jnp.int32) * C_BLOCK
     shift = ((block[:, None] * channel[None, :]) % NCHAN).astype(jnp.float32) * step
-    cos_t = jnp.repeat(jnp.cos(shift), 2, axis=1)
-    sin_t = jnp.repeat(jnp.sin(shift), 2, axis=1)
-    turn = jnp.concatenate([cos_t, sin_t], axis=1)
-    return jnp.concatenate([even, odd], axis=0), jnp.broadcast_to(turn[:, :, None], turn.shape + (128,))
+    turn = jnp.concatenate([jnp.cos(shift), jnp.sin(shift)], axis=1)
+    return first, jnp.broadcast_to(turn[:, :, None], turn.shape + (128,))
 
 
 def channelize_kernel(
-    channels, fold_shift, proto_ref, first_ref, turn_ref, x_hbm, out_ref, buf, sems, acc_ref
+    channels, fold_shift, proto_ref, first_ref, turn_ref, x_hbm, out_ref, buf, sems, acc_ref, *scratch
 ):
     step = pl.program_id(0)
     count = pl.num_programs(0)
@@ -72,10 +68,12 @@
             x_hbm.at[:, :, part, pl.ds(0, cb)], buf.at[slot, part], sems.at[slot, part]
         ).wait()
     turn = jnp.concatenate([turn_ref[...]] * (cb // turn_ref.shape[-1]), axis=1)
-    even, odd = first_ref[: 2 * channels], first_ref[2 * channels :]
-    cos_t, sin_t = turn[: 2 * channels], turn[2 * channels :]
-    upper = even * cos_t - odd * sin_t
-    lower = odd * cos_t + even * sin_t
+    cos_0, sin_0 = first_ref[:channels], first_ref[channels:]
+    cos_t, sin_t = turn[:channels], turn[channels:]
+    cosine = cos_0 * cos_t - sin_0 * sin_t
+    sine = sin_0 * cos_t + cos_0 * sin_t
+    upper = jnp.concatenate([cosine, -sine], axis=0)
+    lower = jnp.concatenate([sine, cosine], axis=0)
     weights = proto_ref[...]
     re_tables = []
     im_tables = []
@@ -117,7 +115,15 @@
             if lead:
                 term = jnp.where(block >= lead, pltpu.roll(term, lead, 0), 0.0)
             total = term if total is None else total + term
-        out_ref[...] = total.T.astype(out_ref.dtype)
+        (staged,) = scratch
+        lanes = staged.shape[-1]
+        for half in range(2):
+            rows_q = pl.ds(half, channels, stride=2)
+            flipped = total[:, half * channels : (half + 1) * channels].T
+            for chunk in range(staged.shape[0]):
+                staged[chunk, rows_q, :] = flipped[:, chunk * lanes : (chunk + 1) * lanes]
+        for chunk in range(staged.shape[0]):
+            out_ref[:, chunk * lanes : (chunk + 1) * lanes] = staged[chunk].astype(out_ref.dtype)
 
 
 def tap_products(voltages, proto, first, turn, channels, fold_shift):
@@ -136,8 +142,8 @@
         grid=(blocks,),
         in_specs=[
             pl.BlockSpec((TAPS, C_BLOCK), lambda j: (0, j)),
-            pl.BlockSpec((4 * channels, C_BLOCK), lambda j: (0, 0)),
-            pl.BlockSpec((None, 4 * channels, 128), lambda j: (j, 0, 0)),
+            pl.BlockSpec((2 * channels, C_BLOCK), lambda j: (0, 0)),
+            pl.BlockSpec((None, 2 * channels, 128), lambda j: (j, 0, 0)),
             pl.BlockSpec(memory_space=pl.ANY),
         ],
         out_specs=pl.BlockSpec(out_shape.shape, lambda j: (0, 0)),
@@ -145,7 +151,8 @@
             pltpu.VMEM((2, 2, local_inputs, time_steps, C_BLOCK), jnp.int32),
             pltpu.SemaphoreType.DMA((2, 2)),
             pltpu.VMEM((rows, width), jnp.float32),
-        ],
+        ]
+        + ([pltpu.VMEM((rows // 128, 2 * channels, 128), jnp.float32)] if fold_shift else []),
         compiler_params=pltpu.CompilerParams(
             dimension_semantics=("arbitrary",), vmem_limit_bytes=48 * 1024 * 1024
         ),
@@ -190,7 +197,7 @@
             for part in range(2):
                 left = lhs_ref[chan, part, rows, :]
                 product = jnp.dot(left, right, preferred_element_type=jnp.float32)
-                out_ref[slot, chan, part] = product * scale
+                out_ref[slot, chan, part] = product
 
 
 def tile_products(spectra, tile_ids, scale):
@@ -199,9 +206,9 @@
     half = depth // 2
     turned_rows = spectra.transpose(0, 2, 1)
     rotated = jnp.concatenate([turned_rows[:, :, half:], -turned_rows[:, :, :half]], axis=2)
-    lhs = jnp.stack([turned_rows, rotated], axis=1)
+    lhs = (jnp.stack([turned_rows, rotated], axis=1) * scale).astype(spectra.dtype)
     count = tile_ids.shape[0]
-    tiles_per_step = max(d for d in range(1, 10) if count % d == 0)
+    tiles_per_step = max(d for d in range(1, 7) if count % d == 0)
     kernel = lambda *refs: correlate_kernel(blocks, tiles_per_step, scale, *refs)
     out_block = (tiles_per_step, local_chans, 2, TB, TB)
     return pl.pallas_call(
@@ -250,7 +257,8 @@
                 [previous[:, tap:, tap], products[:, : time_steps - lead, tap]], axis=1
             )
             total = shifted if total is None else total + shifted
-        spectra = total.astype(jnp.bfloat16).reshape(local_inputs * time_steps, 2 * channels).T
+        spectra = total.reshape(local_inputs * time_steps, 2, channels).transpose(2, 1, 0)
+        spectra = spectra.astype(jnp.bfloat16)
     spectra = spectra.reshape(freq_devices, CH_DEV, 2, local_inputs * time_steps)
     turned = lax.all_to_all(spectra, "freq", split_axis=0, concat_axis=0, tiled=True)
     slot_count = tile_map.shape[0] // time_devices

time: 32.5 us -> 31.6 us (0.972)
  local copies, waits for them, and re-layouts: 2.64 us -> 1.4 us
  Pallas kernels: 13.4 us -> 13.9 us
    another operation x3 -> x0, local copies, waits for them, and re-layouts: 0.88 us -> none  [the longest x1 0.47 us: tile_products(): lhs = jnp.stack([turned_rows, rotated], axis=1)]
    neg x1 -> x0, other arithmetic: 0.6 us -> none  [phase_tables(): even = jnp.stack([cos_0, -sin_0], axis=1).reshape(2 * channels, C_BLOCK)]
    cos x1 -> x2, other arithmetic: 0.12 us -> 0.71 us  [the longest x1 0.59 us: phase_tables(): first = jnp.concatenate([jnp.cos(start), jnp.sin(start)], axis=0)]
    pallas_call x1, Pallas kernels: 5.06 us -> 5.55 us  [tile_products(): pl.pallas_call(kernel, out_shape=jax.ShapeDtypeStruct((count, local_chans...]
    mul x0 -> x1, local copies, waits for them, and re-layouts: none -> 0.47 us  [tile_products(): jnp.stack([turned_rows, rotated], axis=1) * scale]
    reshape x4 -> x0, local copies, waits for them, and re-layouts: 0.46 us -> none  [the longest x1 0.18 us: phase_tables(): even = jnp.stack([cos_0, -sin_0], axis=1).reshape(2 * channels, C_BLOCK)]
where the time goes in v7:
time: 31.6 us; the launch traced here: 31.4 us
  blocking collectives  14.5 us (46%)
  Pallas kernels  13.9 us (44%)
  other arithmetic  1.47 us (5%)
  local copies, waits for them, and re-layouts  1.4 us (4%)
    all_to_all x1, blocking collectives, on_device(): lax.all_to_all(spectra, 'freq', split_axis=0, concat_axis=0, tiled=True)  14.5 us
    pallas_call x1, Pallas kernels, tap_products(): pl.pallas_call(kernel, out_shape=out_shape, grid=(blocks,), in_specs=[pl....  8.34 us
    pallas_call x1, Pallas kernels, tile_products(): pl.pallas_call(kernel, out_shape=jax.ShapeDtypeStruct((count, local_chans...  5.55 us

profile of v7, /device:TPU:0, one launch (start us, length us, event | category | flops | bytes accessed | tf_op | source)
XLA Modules:
  0.0 31.4 jit_solution(9682672514414345367)
XLA Ops:
  0.0 0.0 copy-start
  0.0 0.6 %fusion.12.refs_0_ = f32[4,4096]{1,0:T(4,128)S(1)} fusion(), kind=kLoop, calls=%fused_computation.23 | loop fusion | flops 720896 | bytes 65536 | tf_op jit(solution)/shard_map/div | solution.py:29
  0.6 0.6 %fusion.14 = (f32[64,512]{1,0:T(8,128)S(1)}, f32[64,512]{1,0:T(8,128)S(1)}) fusion(s32[64]{0:T(128)S(1)} %iota_add_fusion), kind=kLoop, calls=%fused_computation.26 | loop fusion | flops 458752 | bytes 262400 | tf_op jit(solution)/shard_map/cos | solution.py:37
  1.2 0.1 fusion.24
  1.4 0.1 pad_maximum_fusion.1
  1.5 0.2 broadcast_in_dim.7.refs_2_
  1.7 8.3 %shard_map.28 = bf16[128,256]{1,0:T(8,128)(2,1)S(1)} custom-call(f32[4,4096]{1,0:T(4,128)S(1)} %fusion.12.refs_0_, f32[128,512]{1,0:T(8,128)S(1)} %pad_maximum_fusion.refs_1_, f32[8,128,128]{2,1,0:T(8,128)S(1)} %broadcast_in_dim.7.refs_2_, s32[32,8,2,4096]{3,2,1,0:T(2,128)} %refs_3_.1), custom_call_target="tpu_custom_call" | custom-call | flops 2147483648 | bytes 9699328 | tf_op jit(solution)/shard_map/pallas_call | solution.py:139
  10.0 14.5 %all_to_all.5 = bf16[32,2,2,256]{3,2,1,0:T(2,128)(2,1)S(1)} all-to-all(bf16[32,2,2,256]{3,2,1,0:T(2,128)(2,1)S(1)} %reshape.22), channel_id=1, replica_groups=mesh['freq'=32,'tm'=1] {'freq'}, dimensions={0} | all-to-all | bytes 131072 | tf_op jit(solution)/shard_map/all_to_all | solution.py:263
  24.6 0.2 copy.7
  24.8 0.2 copy.8
  25.0 0.3 reshape_reshape.3.refs_2_
  25.3 0.5 %copy.9.refs_1_ = bf16[2,2,1024,16]{3,2,1,0:T(8,128)(2,1)S(1)} copy(bf16[2,2,1024,16]{2,3,0,1:T(8,128)(2,1)S(1)} %maximum_multiply_fusion) | data formatting | bytes 262144 | tf_op jit(solution)/shard_map/mul | solution.py:209
  25.8 0.0 copy-done
  25.8 5.6 %shard_map.29 = f32[36,2,2,128,128]{4,3,2,1,0:T(8,128)} custom-call(s32[36]{0:T(128)S(1)} %copy-done, bf16[2,2,1024,16]{3,2,1,0:T(8,128)(2,1)S(1)} %copy.9.refs_1_, bf16[2,16,1024]{2,1,0:T(8,128)(2,1)S(1)} %reshape_reshape.3.refs_2_), custom_call_target="tpu_custom_call" | custom-call | flops 75497472 | bytes 9633792 | tf_op jit(solution)/shard_map/pallas_call | solution.py:214
  (7 shorter events, 0.1 us)
Async XLA Ops:
  0.0 25.8 %copy-start = (s32[36]{0:T(128)S(1)}, s32[36]{0:T(128)}, u32[]{:S(2)}) copy-start(s32[36]{0:T(128)} %refs_0_) | copy-start | bytes 436

commit v8 on v7

--- a/solution.py
+++ b/solution.py
@@ -11,7 +11,7 @@
 TAPS = 4
 TB = 128
 CH_DEV = 2
-C_BLOCK = 512
+C_BLOCK = 1024
 
 
 def passed_along(value, axis, steps):
@@ -208,7 +208,7 @@
     rotated = jnp.concatenate([turned_rows[:, :, half:], -turned_rows[:, :, :half]], axis=2)
     lhs = (jnp.stack([turned_rows, rotated], axis=1) * scale).astype(spectra.dtype)
     count = tile_ids.shape[0]
-    tiles_per_step = max(d for d in range(1, 7) if count % d == 0)
+    tiles_per_step = max(d for d in range(1, 10) if count % d == 0)
     kernel = lambda *refs: correlate_kernel(blocks, tiles_per_step, scale, *refs)
     out_block = (tiles_per_step, local_chans, 2, TB, TB)
     return pl.pallas_call(

time: 31.6 us -> 29.3 us (0.927)
  Pallas kernels: 13.9 us -> 11.1 us
  other arithmetic: 1.47 us -> 2 us
    pallas_call x1, Pallas kernels: 8.34 us -> 6.08 us  [tap_products(): pl.pallas_call(kernel, out_shape=out_shape, grid=(blocks,), in_specs=[pl....]
    cos x1, other arithmetic: 0.59 us -> 1.1 us  [phase_tables(): first = jnp.concatenate([jnp.cos(start), jnp.sin(start)], axis=0)]
    pallas_call x1, Pallas kernels: 5.55 us -> 5.06 us  [tile_products(): pl.pallas_call(kernel, out_shape=jax.ShapeDtypeStruct((count, local_chans...]
where the time goes in v8:
time: 29.3 us; the launch traced here: 29.1 us
  blocking collectives  14.5 us (49%)
  Pallas kernels  11.1 us (38%)
  other arithmetic  2 us (7%)
  local copies, waits for them, and re-layouts  1.33 us (5%)
    all_to_all x1, blocking collectives, on_device(): lax.all_to_all(spectra, 'freq', split_axis=0, concat_axis=0, tiled=True)  14.5 us
    pallas_call x1, Pallas kernels, tap_products(): pl.pallas_call(kernel, out_shape=out_shape, grid=(blocks,), in_specs=[pl....  6.08 us
    pallas_call x1, Pallas kernels, tile_products(): pl.pallas_call(kernel, out_shape=jax.ShapeDtypeStruct((count, local_chans...  5.06 us
    cos x1, other arithmetic, phase_tables(): first = jnp.concatenate([jnp.cos(start), jnp.sin(start)], axis=0)  1.1 us
    div x1, other arithmetic, prototype_rows(): jnp.sinc(position) * hann_taper / (128.0 * math.sqrt(NCHAN))  0.62 us

profile of v8, /device:TPU:0, one launch (start us, length us, event | category | flops | bytes accessed | tf_op | source)
XLA Modules:
  0.0 29.1 jit_solution(10205445267955551333)
XLA Ops:
  0.0 0.0 copy-start
  0.0 0.6 %fusion.14.refs_0_ = f32[4,4096]{1,0:T(4,128)S(1)} fusion(), kind=kLoop, calls=%fused_computation.25 | loop fusion | flops 720896 | bytes 65536 | tf_op jit(solution)/shard_map/div | solution.py:29
  0.6 1.1 %fusion.7 = (f32[64,1024]{1,0:T(8,128)S(1)}, f32[64,1024]{1,0:T(8,128)S(1)}) fusion(s32[64]{0:T(128)S(1)} %iota_add_fusion), kind=kLoop, calls=%fused_computation.12 | loop fusion | flops 917504 | bytes 524544 | tf_op jit(solution)/shard_map/cos | solution.py:37
  1.7 0.1 fusion.24
  1.9 0.1 pad_maximum_fusion.1
  2.0 0.1 broadcast_in_dim.7.refs_2_
  2.1 6.1 %shard_map.28 = bf16[128,256]{1,0:T(8,128)(2,1)S(1)} custom-call(f32[4,4096]{1,0:T(4,128)S(1)} %fusion.14.refs_0_, f32[128,1024]{1,0:T(8,128)S(1)} %pad_maximum_fusion.refs_1_, f32[4,128,128]{2,1,0:T(8,128)S(1)} %broadcast_in_dim.7.refs_2_, s32[32,8,2,4096]{3,2,1,0:T(2,128)} %refs_3_.1), custom_call_target="tpu_custom_call" | custom-call | flops 2147483648 | bytes 9699328 | tf_op jit(solution)/shard_map/pallas_call | solution.py:139
  8.2 14.5 %all_to_all.5 = bf16[32,2,2,256]{3,2,1,0:T(2,128)(2,1)S(1)} all-to-all(bf16[32,2,2,256]{3,2,1,0:T(2,128)(2,1)S(1)} %reshape.22), channel_id=1, replica_groups=mesh['freq'=32,'tm'=1] {'freq'}, dimensions={0} | all-to-all | bytes 131072 | tf_op jit(solution)/shard_map/all_to_all | solution.py:263
  22.8 0.2 copy.7
  23.0 0.2 copy.8
  23.2 0.3 reshape_reshape.3.refs_2_
  23.5 0.5 %copy.9.refs_1_ = bf16[2,2,1024,16]{3,2,1,0:T(8,128)(2,1)S(1)} copy(bf16[2,2,1024,16]{2,3,0,1:T(8,128)(2,1)S(1)} %maximum_multiply_fusion) | data formatting | bytes 262144 | tf_op jit(solution)/shard_map/mul | solution.py:209
  24.0 0.0 copy-done
  24.0 5.1 %shard_map.29 = f32[36,2,2,128,128]{4,3,2,1,0:T(8,128)} custom-call(s32[36]{0:T(128)S(1)} %copy-done, bf16[2,2,1024,16]{3,2,1,0:T(8,128)(2,1)S(1)} %copy.9.refs_1_, bf16[2,16,1024]{2,1,0:T(8,128)(2,1)S(1)} %reshape_reshape.3.refs_2_), custom_call_target="tpu_custom_call" | custom-call | flops 75497472 | bytes 9633792 | tf_op jit(solution)/shard_map/pallas_call | solution.py:214
  (7 shorter events, 0.1 us)
Async XLA Ops:
  0.0 24.0 %copy-start = (s32[36]{0:T(128)S(1)}, s32[36]{0:T(128)}, u32[]{:S(2)}) copy-start(s32[36]{0:T(128)} %refs_0_) | copy-start | bytes 436

commit v9 on v8

--- a/solution.py
+++ b/solution.py
@@ -12,6 +12,7 @@
 TB = 128
 CH_DEV = 2
 C_BLOCK = 1024
+LANES = 128
 
 
 def passed_along(value, axis, steps):
@@ -32,13 +33,12 @@
 def phase_tables(first_channel, channels):
     channel = first_channel + jnp.arange(channels, dtype=jnp.int32)
     step = 2.0 * math.pi / NCHAN
-    lane = jnp.arange(C_BLOCK, dtype=jnp.int32)
+    lane = jnp.arange(LANES, dtype=jnp.int32)
     start = ((lane[None, :] * channel[:, None]) % NCHAN).astype(jnp.float32) * step
     first = jnp.concatenate([jnp.cos(start), jnp.sin(start)], axis=0)
-    block = jnp.arange(NCHAN // C_BLOCK, dtype=jnp.int32) * C_BLOCK
-    shift = ((block[:, None] * channel[None, :]) % NCHAN).astype(jnp.float32) * step
-    turn = jnp.concatenate([jnp.cos(shift), jnp.sin(shift)], axis=1)
-    return first, jnp.broadcast_to(turn[:, :, None], turn.shape + (128,))
+    chunk = jnp.arange(NCHAN // LANES, dtype=jnp.int32) * LANES
+    shift = ((chunk[:, None] * channel[None, :]) % NCHAN).astype(jnp.float32) * step
+    return first, jnp.concatenate([jnp.cos(shift), jnp.sin(shift)], axis=1)
 
 
 def channelize_kernel(
@@ -67,11 +67,16 @@
         pltpu.make_async_copy(
             x_hbm.at[:, :, part, pl.ds(0, cb)], buf.at[slot, part], sems.at[slot, part]
         ).wait()
-    turn = jnp.concatenate([turn_ref[...]] * (cb // turn_ref.shape[-1]), axis=1)
+    turn = turn_ref[...].T
     cos_0, sin_0 = first_ref[:channels], first_ref[channels:]
-    cos_t, sin_t = turn[:channels], turn[channels:]
-    cosine = cos_0 * cos_t - sin_0 * sin_t
-    sine = sin_0 * cos_t + cos_0 * sin_t
+    cos_parts, sin_parts = [], []
+    for chunk in range(cb // LANES):
+        cos_t = jnp.broadcast_to(turn[:channels, chunk : chunk + 1], cos_0.shape)
+        sin_t = jnp.broadcast_to(turn[channels:, chunk : chunk + 1], cos_0.shape)
+        cos_parts.append(cos_0 * cos_t - sin_0 * sin_t)
+        sin_parts.append(sin_0 * cos_t + cos_0 * sin_t)
+    cosine = jnp.concatenate(cos_parts, axis=1)
+    sine = jnp.concatenate(sin_parts, axis=1)
     upper = jnp.concatenate([cosine, -sine], axis=0)
     lower = jnp.concatenate([sine, cosine], axis=0)
     weights = proto_ref[...]
@@ -142,8 +147,8 @@
         grid=(blocks,),
         in_specs=[
             pl.BlockSpec((TAPS, C_BLOCK), lambda j: (0, j)),
-            pl.BlockSpec((2 * channels, C_BLOCK), lambda j: (0, 0)),
-            pl.BlockSpec((None, 2 * channels, 128), lambda j: (j, 0, 0)),
+            pl.BlockSpec((2 * channels, LANES), lambda j: (0, 0)),
+            pl.BlockSpec((C_BLOCK // LANES, 2 * channels), lambda j: (j, 0)),
             pl.BlockSpec(memory_space=pl.ANY),
         ],
         out_specs=pl.BlockSpec(out_shape.shape, lambda j: (0, 0)),

time: 29.3 us -> 28.8 us (0.983)
  other arithmetic: 2 us -> 1.11 us
  Pallas kernels: 11.1 us -> 11.7 us
    cos x1, other arithmetic: 1.1 us -> 0.21 us  [phase_tables(): first = jnp.concatenate([jnp.cos(start), jnp.sin(start)], axis=0)]
    pallas_call x1, Pallas kernels: 6.08 us -> 6.63 us  [tap_products(): pl.pallas_call(kernel, out_shape=out_shape, grid=(blocks,), in_specs=[pl....]
where the time goes in v9:
time: 28.8 us; the launch traced here: 28.6 us
  blocking collectives  14.5 us (50%)
  Pallas kernels  11.7 us (41%)
  local copies, waits for them, and re-layouts  1.21 us (4%)
  other arithmetic  1.11 us (4%)
    all_to_all x1, blocking collectives, on_device(): lax.all_to_all(spectra, 'freq', split_axis=0, concat_axis=0, tiled=True)  14.5 us
    pallas_call x1, Pallas kernels, tap_products(): pl.pallas_call(kernel, out_shape=out_shape, grid=(blocks,), in_specs=[pl....  6.63 us
    pallas_call x1, Pallas kernels, tile_products(): pl.pallas_call(kernel, out_shape=jax.ShapeDtypeStruct((count, local_chans...  5.06 us
    div x1, other arithmetic, prototype_rows(): jnp.sinc(position) * hann_taper / (128.0 * math.sqrt(NCHAN))  0.62 us

profile of v9, /device:TPU:0, one launch (start us, length us, event | category | flops | bytes accessed | tf_op | source)
XLA Modules:
  0.0 28.6 jit_solution(1434261895802086243)
XLA Ops:
  0.0 0.0 copy-start
  0.0 0.6 %fusion.6.refs_0_ = f32[4,4096]{1,0:T(4,128)S(1)} fusion(), kind=kLoop, calls=%fused_computation.13 | loop fusion | flops 720896 | bytes 65536 | tf_op jit(solution)/shard_map/div | solution.py:30
  0.6 0.2 fusion.22
  0.8 0.2 fusion.24
  1.0 0.1 pad_maximum_fusion.1.refs_2_
  1.1 6.6 %shard_map.28 = bf16[128,256]{1,0:T(8,128)(2,1)S(1)} custom-call(f32[4,4096]{1,0:T(4,128)S(1)} %fusion.6.refs_0_, f32[128,128]{1,0:T(8,128)S(1)} %pad_maximum_fusion.refs_1_, f32[32,128]{1,0:T(8,128)S(1)} %pad_maximum_fusion.1.refs_2_, s32[32,8,2,4096]{3,2,1,0:T(2,128)} %refs_3_.1), custom_call_target="tpu_custom_call" | custom-call | flops 2147483648 | bytes 8994816 | tf_op jit(solution)/shard_map/pallas_call | solution.py:144
  7.8 14.5 %all_to_all.5 = bf16[32,2,2,256]{3,2,1,0:T(2,128)(2,1)S(1)} all-to-all(bf16[32,2,2,256]{3,2,1,0:T(2,128)(2,1)S(1)} %reshape.21), channel_id=1, replica_groups=mesh['freq'=32,'tm'=1] {'freq'}, dimensions={0} | all-to-all | bytes 131072 | tf_op jit(solution)/shard_map/all_to_all | solution.py:268
  22.3 0.2 copy.7
  22.5 0.2 copy.8
  22.7 0.3 reshape_reshape.3.refs_2_
  23.1 0.5 %copy.9.refs_1_ = bf16[2,2,1024,16]{3,2,1,0:T(8,128)(2,1)S(1)} copy(bf16[2,2,1024,16]{2,3,0,1:T(8,128)(2,1)S(1)} %maximum_multiply_fusion) | data formatting | bytes 262144 | tf_op jit(solution)/shard_map/mul | solution.py:214
  23.6 0.0 copy-done
  23.6 5.1 %shard_map.29 = f32[36,2,2,128,128]{4,3,2,1,0:T(8,128)} custom-call(s32[36]{0:T(128)S(1)} %copy-done, bf16[2,2,1024,16]{3,2,1,0:T(8,128)(2,1)S(1)} %copy.9.refs_1_, bf16[2,16,1024]{2,1,0:T(8,128)(2,1)S(1)} %reshape_reshape.3.refs_2_), custom_call_target="tpu_custom_call" | custom-call | flops 75497472 | bytes 9633792 | tf_op jit(solution)/shard_map/pallas_call | solution.py:219
  (7 shorter events, 0.1 us)
Async XLA Ops:
  0.0 23.6 %copy-start = (s32[36]{0:T(128)S(1)}, s32[36]{0:T(128)}, u32[]{:S(2)}) copy-start(s32[36]{0:T(128)} %refs_0_) | copy-start | bytes 436

commit v10 on v9

--- a/solution.py
+++ b/solution.py
@@ -187,22 +187,31 @@
     return unfolded.reshape(local_chans, 2, piece_count * time_steps, freq_count * inner_width)
 
 
-def correlate_kernel(blocks, tiles_per_step, scale, ids_ref, lhs_ref, rhs_ref, out_ref):
-    step = pl.program_id(0)
-    for slot in range(tiles_per_step):
-        tile_id = ids_ref[step * tiles_per_step + slot]
-        row_block = jnp.int32(0)
-        for r in range(1, blocks):
-            row_block = row_block + (tile_id >= r * (r + 1) // 2).astype(jnp.int32)
-        col_block = tile_id - row_block * (row_block + 1) // 2
-        rows = pl.ds(pl.multiple_of(row_block * TB, TB), TB)
-        cols = pl.ds(pl.multiple_of(col_block * TB, TB), TB)
-        for chan in range(lhs_ref.shape[0]):
-            right = rhs_ref[chan, :, cols]
-            for part in range(2):
-                left = lhs_ref[chan, part, rows, :]
-                product = jnp.dot(left, right, preferred_element_type=jnp.float32)
-                out_ref[slot, chan, part] = product
+def correlate_kernel(blocks, groups, ids_ref, lhs_ref, rhs_ref, out_hbm, staged, sems):
+    count = staged.shape[0]
+    per_group = count // groups
+
+    def copy(group):
+        part = pl.ds(group * per_group, per_group)
+        return pltpu.make_async_copy(staged.at[part], out_hbm.at[part], sems.at[group])
+
+    for group in range(groups):
+        for slot in range(group * per_group, (group + 1) * per_group):
+            tile_id = ids_ref[slot]
+            row_block = jnp.int32(0)
+            for r in range(1, blocks):
+                row_block = row_block + (tile_id >= r * (r + 1) // 2).astype(jnp.int32)
+            col_block = tile_id - row_block * (row_block + 1) // 2
+            rows = pl.ds(pl.multiple_of(row_block * TB, TB), TB)
+            cols = pl.ds(pl.multiple_of(col_block * TB, TB), TB)
+            for chan in range(lhs_ref.shape[0]):
+                right = rhs_ref[chan, :, cols]
+                for part in range(2):
+                    left = lhs_ref[chan, part, rows, :]
+                    staged[slot, chan, part] = jnp.dot(left, right, preferred_element_type=jnp.float32)
+        copy(group).start()
+    for group in range(groups):
+        copy(group).wait()
 
 
 def tile_products(spectra, tile_ids, scale):
@@ -213,24 +222,20 @@
     rotated = jnp.concatenate([turned_rows[:, :, half:], -turned_rows[:, :, :half]], axis=2)
     lhs = (jnp.stack([turned_rows, rotated], axis=1) * scale).astype(spectra.dtype)
     count = tile_ids.shape[0]
-    tiles_per_step = max(d for d in range(1, 10) if count % d == 0)
-    kernel = lambda *refs: correlate_kernel(blocks, tiles_per_step, scale, *refs)
-    out_block = (tiles_per_step, local_chans, 2, TB, TB)
+    groups = max(d for d in range(1, 5) if count % d == 0)
+    kernel = lambda *refs: correlate_kernel(blocks, groups, *refs)
+    out_shape = (count, local_chans, 2, TB, TB)
     return pl.pallas_call(
         kernel,
-        out_shape=jax.ShapeDtypeStruct((count, local_chans, 2, TB, TB), jnp.float32),
-        grid_spec=pltpu.PrefetchScalarGridSpec(
-            num_scalar_prefetch=1,
-            grid=(count // tiles_per_step,),
-            in_specs=[
-                pl.BlockSpec(lhs.shape, lambda j, ids: (0, 0, 0, 0)),
-                pl.BlockSpec(spectra.shape, lambda j, ids: (0, 0, 0)),
-            ],
-            out_specs=pl.BlockSpec(out_block, lambda j, ids: (j, 0, 0, 0, 0)),
-        ),
-        compiler_params=pltpu.CompilerParams(
-            dimension_semantics=("arbitrary",), vmem_limit_bytes=48 * 1024 * 1024
-        ),
+        out_shape=jax.ShapeDtypeStruct(out_shape, jnp.float32),
+        in_specs=[
+            pl.BlockSpec(memory_space=pltpu.SMEM),
+            pl.BlockSpec(memory_space=pltpu.VMEM),
+            pl.BlockSpec(memory_space=pltpu.VMEM),
+        ],
+        out_specs=pl.BlockSpec(memory_space=pl.ANY),
+        scratch_shapes=[pltpu.VMEM(out_shape, jnp.float32), pltpu.SemaphoreType.DMA((groups,))],
+        compiler_params=pltpu.CompilerParams(vmem_limit_bytes=48 * 1024 * 1024),
         cost_estimate=pl.CostEstimate(
             flops=2 * count * local_chans * 2 * TB * TB * depth,
             transcendentals=0,

time: 28.8 us -> 28.4 us (0.986)
  Pallas kernels: 11.7 us -> 11.3 us
    pallas_call x1, Pallas kernels: 5.06 us -> 4.7 us  [tile_products(): pl.pallas_call(kernel, out_shape=jax.ShapeDtypeStruct(out_shape, jnp.floa...]
where the time goes in v10:
time: 28.4 us; the launch traced here: 28.3 us
  blocking collectives  14.5 us (51%)
  Pallas kernels  11.3 us (40%)
  local copies, waits for them, and re-layouts  1.21 us (4%)
  other arithmetic  1.11 us (4%)
    all_to_all x1, blocking collectives, on_device(): lax.all_to_all(spectra, 'freq', split_axis=0, concat_axis=0, tiled=True)  14.5 us
    pallas_call x1, Pallas kernels, tap_products(): pl.pallas_call(kernel, out_shape=out_shape, grid=(blocks,), in_specs=[pl....  6.63 us
    pallas_call x1, Pallas kernels, tile_products(): pl.pallas_call(kernel, out_shape=jax.ShapeDtypeStruct(out_shape, jnp.floa...  4.7 us
    div x1, other arithmetic, prototype_rows(): jnp.sinc(position) * hann_taper / (128.0 * math.sqrt(NCHAN))  0.62 us

profile of v10, /device:TPU:0, one launch (start us, length us, event | category | flops | bytes accessed | tf_op | source)
XLA Modules:
  0.0 28.3 jit_solution(5624267095840031819)
XLA Ops:
  0.0 0.0 copy-start
  0.0 0.6 %fusion.6.refs_0_ = f32[4,4096]{1,0:T(4,128)S(1)} fusion(), kind=kLoop, calls=%fused_computation.13 | loop fusion | flops 720896 | bytes 65536 | tf_op jit(solution)/shard_map/div | solution.py:30
  0.6 0.2 fusion.22
  0.8 0.2 fusion.24
  1.0 0.1 pad_maximum_fusion.1.refs_2_
  1.1 6.6 %shard_map.28 = bf16[128,256]{1,0:T(8,128)(2,1)S(1)} custom-call(f32[4,4096]{1,0:T(4,128)S(1)} %fusion.6.refs_0_, f32[128,128]{1,0:T(8,128)S(1)} %pad_maximum_fusion.refs_1_, f32[32,128]{1,0:T(8,128)S(1)} %pad_maximum_fusion.1.refs_2_, s32[32,8,2,4096]{3,2,1,0:T(2,128)} %refs_3_.1), custom_call_target="tpu_custom_call" | custom-call | flops 2147483648 | bytes 8994816 | tf_op jit(solution)/shard_map/pallas_call | solution.py:144
  7.8 14.5 %all_to_all.5 = bf16[32,2,2,256]{3,2,1,0:T(2,128)(2,1)S(1)} all-to-all(bf16[32,2,2,256]{3,2,1,0:T(2,128)(2,1)S(1)} %reshape.21), channel_id=1, replica_groups=mesh['freq'=32,'tm'=1] {'freq'}, dimensions={0} | all-to-all | bytes 131072 | tf_op jit(solution)/shard_map/all_to_all | solution.py:273
  22.3 0.2 copy.7
  22.5 0.2 copy.8
  22.7 0.3 reshape_reshape.3.refs_2_
  23.1 0.5 %copy.9.refs_1_ = bf16[2,2,1024,16]{3,2,1,0:T(8,128)(2,1)S(1)} copy(bf16[2,2,1024,16]{2,3,0,1:T(8,128)(2,1)S(1)} %maximum_multiply_fusion) | data formatting | bytes 262144 | tf_op jit(solution)/shard_map/mul | solution.py:223
  23.6 0.0 copy-done
  23.6 4.7 %shard_map.29 = f32[36,2,2,128,128]{4,3,2,1,0:T(8,128)} custom-call(s32[36]{0:T(128)S(1)} %copy-done, bf16[2,2,1024,16]{3,2,1,0:T(8,128)(2,1)S(1)} %copy.9.refs_1_, bf16[2,16,1024]{2,1,0:T(8,128)(2,1)S(1)} %reshape_reshape.3.refs_2_), custom_call_target="tpu_custom_call" | custom-call | flops 75497472 | bytes 9633792 | tf_op jit(solution)/shard_map/pallas_call | solution.py:228
  (7 shorter events, 0.1 us)
Async XLA Ops:
  0.0 23.6 %copy-start = (s32[36]{0:T(128)S(1)}, s32[36]{0:T(128)}, u32[]{:S(2)}) copy-start(s32[36]{0:T(128)} %refs_0_) | copy-start | bytes 436

commit v11 on v10

--- a/solution.py
+++ b/solution.py
@@ -11,7 +11,7 @@
 TAPS = 4
 TB = 128
 CH_DEV = 2
-C_BLOCK = 1024
+C_BLOCK = 2048
 LANES = 128
 
 

time: 28.4 us -> 27.4 us (0.965)
  Pallas kernels: 11.3 us -> 10.3 us
    pallas_call x1, Pallas kernels: 6.63 us -> 5.64 us  [tap_products(): pl.pallas_call(kernel, out_shape=out_shape, grid=(blocks,), in_specs=[pl....]
where the time goes in v11:
time: 27.4 us; the launch traced here: 27.3 us
  blocking collectives  14.5 us (53%)
  Pallas kernels  10.3 us (38%)
  local copies, waits for them, and re-layouts  1.21 us (4%)
  other arithmetic  1.11 us (4%)
    all_to_all x1, blocking collectives, on_device(): lax.all_to_all(spectra, 'freq', split_axis=0, concat_axis=0, tiled=True)  14.5 us
    pallas_call x1, Pallas kernels, tap_products(): pl.pallas_call(kernel, out_shape=out_shape, grid=(blocks,), in_specs=[pl....  5.64 us
    pallas_call x1, Pallas kernels, tile_products(): pl.pallas_call(kernel, out_shape=jax.ShapeDtypeStruct(out_shape, jnp.floa...  4.7 us
    div x1, other arithmetic, prototype_rows(): jnp.sinc(position) * hann_taper / (128.0 * math.sqrt(NCHAN))  0.62 us

profile of v11, /device:TPU:0, one launch (start us, length us, event | category | flops | bytes accessed | tf_op | source)
XLA Modules:
  0.0 27.3 jit_solution(10367575736439175543)
XLA Ops:
  0.0 0.0 copy-start
  0.0 0.6 %fusion.6.refs_0_ = f32[4,4096]{1,0:T(4,128)S(1)} fusion(), kind=kLoop, calls=%fused_computation.13 | loop fusion | flops 720896 | bytes 65536 | tf_op jit(solution)/shard_map/div | solution.py:30
  0.6 0.2 fusion.22
  0.8 0.2 fusion.24
  1.0 0.1 pad_maximum_fusion.1.refs_2_
  1.1 5.6 %shard_map.28 = bf16[128,256]{1,0:T(8,128)(2,1)S(1)} custom-call(f32[4,4096]{1,0:T(4,128)S(1)} %fusion.6.refs_0_, f32[128,128]{1,0:T(8,128)S(1)} %pad_maximum_fusion.refs_1_, f32[32,128]{1,0:T(8,128)S(1)} %pad_maximum_fusion.1.refs_2_, s32[32,8,2,4096]{3,2,1,0:T(2,128)} %refs_3_.1), custom_call_target="tpu_custom_call" | custom-call | flops 2147483648 | bytes 8994816 | tf_op jit(solution)/shard_map/pallas_call | solution.py:144
  6.8 14.5 %all_to_all.5 = bf16[32,2,2,256]{3,2,1,0:T(2,128)(2,1)S(1)} all-to-all(bf16[32,2,2,256]{3,2,1,0:T(2,128)(2,1)S(1)} %reshape.21), channel_id=1, replica_groups=mesh['freq'=32,'tm'=1] {'freq'}, dimensions={0} | all-to-all | bytes 131072 | tf_op jit(solution)/shard_map/all_to_all | solution.py:273
  21.3 0.2 copy.7
  21.5 0.2 copy.8
  21.7 0.3 %reshape_reshape.3.refs_2_ = bf16[2,16,1024]{2,1,0:T(8,128)(2,1)S(1)} reshape(bf16[2,2,1,8,32,32]{5,4,3,1,0,2:T(8,128)(2,1)S(1)} %copy.8) | data formatting | bytes 131072 | tf_op jit(solution)/shard_map/reshape;reshape | solution.py:278
  22.1 0.5 %copy.9.refs_1_ = bf16[2,2,1024,16]{3,2,1,0:T(8,128)(2,1)S(1)} copy(bf16[2,2,1024,16]{2,3,0,1:T(8,128)(2,1)S(1)} %maximum_multiply_fusion) | data formatting | bytes 262144 | tf_op jit(solution)/shard_map/mul | solution.py:223
  22.6 0.0 copy-done
  22.6 4.7 %shard_map.29 = f32[36,2,2,128,128]{4,3,2,1,0:T(8,128)} custom-call(s32[36]{0:T(128)S(1)} %copy-done, bf16[2,2,1024,16]{3,2,1,0:T(8,128)(2,1)S(1)} %copy.9.refs_1_, bf16[2,16,1024]{2,1,0:T(8,128)(2,1)S(1)} %reshape_reshape.3.refs_2_), custom_call_target="tpu_custom_call" | custom-call | flops 75497472 | bytes 9633792 | tf_op jit(solution)/shard_map/pallas_call | solution.py:228
  (7 shorter events, 0.1 us)
Async XLA Ops:
  0.0 22.6 %copy-start = (s32[36]{0:T(128)S(1)}, s32[36]{0:T(128)}, u32[]{:S(2)}) copy-start(s32[36]{0:T(128)} %refs_0_) | copy-start | bytes 436

commit v12 on v11

--- a/solution.py
+++ b/solution.py
@@ -21,28 +21,19 @@
     return lax.ppermute(value, axis, [(source, source + steps) for source in range(leading, last)])
 
 
-def prototype_rows():
-    sample_idx = jnp.arange(TAPS * NCHAN, dtype=jnp.int32)
-    position = (sample_idx.astype(jnp.float32) + 0.5) / NCHAN - TAPS / 2.0
-    hann_taper = 0.5 - 0.5 * jnp.cos(
-        (sample_idx.astype(jnp.float32) + 0.5) * (2.0 * math.pi / (TAPS * NCHAN))
-    )
-    return (jnp.sinc(position) * hann_taper / (128.0 * math.sqrt(NCHAN))).reshape(TAPS, NCHAN)
-
-
-def phase_tables(first_channel, channels):
-    channel = first_channel + jnp.arange(channels, dtype=jnp.int32)
-    step = 2.0 * math.pi / NCHAN
-    lane = jnp.arange(LANES, dtype=jnp.int32)
-    start = ((lane[None, :] * channel[:, None]) % NCHAN).astype(jnp.float32) * step
-    first = jnp.concatenate([jnp.cos(start), jnp.sin(start)], axis=0)
-    chunk = jnp.arange(NCHAN // LANES, dtype=jnp.int32) * LANES
-    shift = ((chunk[:, None] * channel[None, :]) % NCHAN).astype(jnp.float32) * step
-    return first, jnp.concatenate([jnp.cos(shift), jnp.sin(shift)], axis=1)
-
-
 def channelize_kernel(
-    channels, fold_shift, proto_ref, first_ref, turn_ref, x_hbm, out_ref, buf, sems, acc_ref, *scratch
+    channels,
+    first_channel,
+    fold_shift,
+    x_hbm,
+    out_ref,
+    buf,
+    sems,
+    acc_ref,
+    proto_ref,
+    first_ref,
+    turn_ref,
+    *scratch,
 ):
     step = pl.program_id(0)
     count = pl.num_programs(0)
@@ -57,6 +48,26 @@
     @pl.when(step == 0)
     def _():
         fetch(0, 0)
+        sample = (
+            lax.broadcasted_iota(jnp.int32, proto_ref.shape, 0) * NCHAN
+            + lax.broadcasted_iota(jnp.int32, proto_ref.shape, 1)
+        ).astype(jnp.float32)
+        position = (sample + 0.5) / NCHAN - TAPS / 2.0
+        hann_taper = 0.5 - 0.5 * jnp.cos((sample + 0.5) * (2.0 * math.pi / (TAPS * NCHAN)))
+        pi_x = math.pi * position
+        proto_ref[...] = jnp.sin(pi_x) / pi_x * hann_taper / (128.0 * math.sqrt(NCHAN))
+        angle = 2.0 * math.pi / NCHAN
+        row = lax.broadcasted_iota(jnp.int32, (channels, LANES), 0) + first_channel
+        lane = lax.broadcasted_iota(jnp.int32, (channels, LANES), 1)
+        start = jnp.bitwise_and(lane * row, NCHAN - 1).astype(jnp.float32) * angle
+        first_ref[:channels] = jnp.cos(start)
+        first_ref[channels:] = jnp.sin(start)
+        chunks = turn_ref.shape[0]
+        chunk = lax.broadcasted_iota(jnp.int32, (chunks, channels), 0) * LANES
+        col = lax.broadcasted_iota(jnp.int32, (chunks, channels), 1) + first_channel
+        shift = jnp.bitwise_and(chunk * col, NCHAN - 1).astype(jnp.float32) * angle
+        turn_ref[:, :channels] = jnp.cos(shift)
+        turn_ref[:, channels:] = jnp.sin(shift)
 
     @pl.when(step + 1 < count)
     def _():
@@ -67,7 +78,8 @@
         pltpu.make_async_copy(
             x_hbm.at[:, :, part, pl.ds(0, cb)], buf.at[slot, part], sems.at[slot, part]
         ).wait()
-    turn = turn_ref[...].T
+    per_block = cb // LANES
+    turn = turn_ref[pl.ds(pl.multiple_of(step * per_block, per_block), per_block), :].T
     cos_0, sin_0 = first_ref[:channels], first_ref[channels:]
     cos_parts, sin_parts = [], []
     for chunk in range(cb // LANES):
@@ -79,7 +91,7 @@
     sine = jnp.concatenate(sin_parts, axis=1)
     upper = jnp.concatenate([cosine, -sine], axis=0)
     lower = jnp.concatenate([sine, cosine], axis=0)
-    weights = proto_ref[...]
+    weights = proto_ref[:, pl.ds(pl.multiple_of(step * cb, cb), cb)]
     re_tables = []
     im_tables = []
     for tap in range(TAPS):
@@ -131,12 +143,12 @@
             out_ref[:, chunk * lanes : (chunk + 1) * lanes] = staged[chunk].astype(out_ref.dtype)
 
 
-def tap_products(voltages, proto, first, turn, channels, fold_shift):
+def tap_products(voltages, first_channel, channels, fold_shift):
     local_inputs, time_steps = voltages.shape[0], voltages.shape[1]
     rows = local_inputs * time_steps
     width = TAPS * 2 * channels
     blocks = NCHAN // C_BLOCK
-    kernel = lambda *refs: channelize_kernel(channels, fold_shift, *refs)
+    kernel = lambda *refs: channelize_kernel(channels, first_channel, fold_shift, *refs)
     if fold_shift:
         out_shape = jax.ShapeDtypeStruct((2 * channels, rows), jnp.bfloat16)
     else:
@@ -145,17 +157,15 @@
         kernel,
         out_shape=out_shape,
         grid=(blocks,),
-        in_specs=[
-            pl.BlockSpec((TAPS, C_BLOCK), lambda j: (0, j)),
-            pl.BlockSpec((2 * channels, LANES), lambda j: (0, 0)),
-            pl.BlockSpec((C_BLOCK // LANES, 2 * channels), lambda j: (j, 0)),
-            pl.BlockSpec(memory_space=pl.ANY),
-        ],
+        in_specs=[pl.BlockSpec(memory_space=pl.ANY)],
         out_specs=pl.BlockSpec(out_shape.shape, lambda j: (0, 0)),
         scratch_shapes=[
             pltpu.VMEM((2, 2, local_inputs, time_steps, C_BLOCK), jnp.int32),
             pltpu.SemaphoreType.DMA((2, 2)),
             pltpu.VMEM((rows, width), jnp.float32),
+            pltpu.VMEM((TAPS, NCHAN), jnp.float32),
+            pltpu.VMEM((2 * channels, LANES), jnp.float32),
+            pltpu.VMEM((NCHAN // LANES, 2 * channels), jnp.float32),
         ]
         + ([pltpu.VMEM((rows // 128, 2 * channels, 128), jnp.float32)] if fold_shift else []),
         compiler_params=pltpu.CompilerParams(
@@ -164,9 +174,9 @@
         cost_estimate=pl.CostEstimate(
             flops=2 * rows * 2 * NCHAN * width,
             transcendentals=0,
-            bytes_accessed=voltages.size * 4 + rows * width * 4 + first.size * 4 + turn.size * 4,
+            bytes_accessed=voltages.size * 4 + rows * width * 4,
         ),
-    )(proto, first, turn, voltages)
+    )(voltages)
 
 
 def tile_coords(tile_id, blocks):
@@ -251,12 +261,10 @@
     time_devices = lax.axis_size("tm")
     channels = CH_DEV * freq_devices
     first_channel = NCHAN // 2 - channels // 2
-    proto = prototype_rows()
-    first, turn = phase_tables(first_channel, channels)
     if time_devices == 1:
-        spectra = tap_products(voltages, proto, first, turn, channels, True)
+        spectra = tap_products(voltages, first_channel, channels, True)
     else:
-        products = tap_products(voltages, proto, first, turn, channels, False)
+        products = tap_products(voltages, first_channel, channels, False)
         products = products.reshape(local_inputs, time_steps, TAPS, 2 * channels)
         tail = products[:, time_steps - (TAPS - 1) :]
         previous = passed_along(tail, "tm", 1)

time: 27.4 us -> 26.3 us (0.960)
  other arithmetic: 1.11 us -> 0.04 us
    div x1 -> x0, other arithmetic: 0.62 us -> none  [prototype_rows(): jnp.sinc(position) * hann_taper / (128.0 * math.sqrt(NCHAN))]
    cos x2 -> x0, other arithmetic: 0.36 us -> none  [the longest x1 0.21 us: phase_tables(): first = jnp.concatenate([jnp.cos(start), jnp.sin(start)], axis=0)]
where the time goes in v12:
time: 26.3 us; the launch traced here: 26.2 us
  blocking collectives  14.5 us (55%)
  Pallas kernels  10.3 us (39%)
  local copies, waits for them, and re-layouts  1.21 us (5%)
    all_to_all x1, blocking collectives, on_device(): lax.all_to_all(spectra, 'freq', split_axis=0, concat_axis=0, tiled=True)  14.5 us
    pallas_call x1, Pallas kernels, tap_products(): pl.pallas_call(kernel, out_shape=out_shape, grid=(blocks,), in_specs=[pl....  5.65 us
    pallas_call x1, Pallas kernels, tile_products(): pl.pallas_call(kernel, out_shape=jax.ShapeDtypeStruct(out_shape, jnp.floa...  4.7 us

profile of v12, /device:TPU:0, one launch (start us, length us, event | category | flops | bytes accessed | tf_op | source)
XLA Modules:
  0.0 26.2 jit_solution(12286850499995873274)
XLA Ops:
  0.0 0.0 copy-start
  0.0 5.6 %shard_map.28 = bf16[128,256]{1,0:T(8,128)(2,1)S(1)} custom-call(s32[32,8,2,4096]{3,2,1,0:T(2,128)} %refs_0_.1), custom_call_target="tpu_custom_call" | custom-call | flops 2147483648 | bytes 8912896 | tf_op jit(solution)/shard_map/pallas_call | solution.py:156
  5.7 14.5 %all_to_all.5 = bf16[32,2,2,256]{3,2,1,0:T(2,128)(2,1)S(1)} all-to-all(bf16[32,2,2,256]{3,2,1,0:T(2,128)(2,1)S(1)} %reshape.7), channel_id=1, replica_groups=mesh['freq'=32,'tm'=1] {'freq'}, dimensions={0} | all-to-all | bytes 131072 | tf_op jit(solution)/shard_map/all_to_all | solution.py:281
  20.2 0.2 copy.7
  20.4 0.2 copy.8
  20.7 0.3 %reshape_reshape.3.refs_2_ = bf16[2,16,1024]{2,1,0:T(8,128)(2,1)S(1)} reshape(bf16[2,2,1,8,32,32]{5,4,3,1,0,2:T(8,128)(2,1)S(1)} %copy.8) | data formatting | bytes 131072 | tf_op jit(solution)/shard_map/reshape;reshape | solution.py:286
  21.0 0.5 %copy.9.refs_1_ = bf16[2,2,1024,16]{3,2,1,0:T(8,128)(2,1)S(1)} copy(bf16[2,2,1024,16]{2,3,0,1:T(8,128)(2,1)S(1)} %maximum_multiply_fusion) | data formatting | bytes 262144 | tf_op jit(solution)/shard_map/mul | solution.py:233
  21.5 0.0 copy-done
  21.5 4.7 %shard_map.29 = f32[36,2,2,128,128]{4,3,2,1,0:T(8,128)} custom-call(s32[36]{0:T(128)S(1)} %copy-done, bf16[2,2,1024,16]{3,2,1,0:T(8,128)(2,1)S(1)} %copy.9.refs_1_, bf16[2,16,1024]{2,1,0:T(8,128)(2,1)S(1)} %reshape_reshape.3.refs_2_), custom_call_target="tpu_custom_call" | custom-call | flops 75497472 | bytes 9633792 | tf_op jit(solution)/shard_map/pallas_call | solution.py:238
  (4 shorter events, 0.1 us)
Async XLA Ops:
  0.0 21.5 %copy-start = (s32[36]{0:T(128)S(1)}, s32[36]{0:T(128)}, u32[]{:S(2)}) copy-start(s32[36]{0:T(128)} %refs_0_.2) | copy-start | bytes 436
